TPU v7x, 32 devices: a whole 2x2x4 slice. The times are simulated.
32 devices in a mesh: seq: 4 (over z), crow: 4 (over y, x), ccol: 2 (over core).
Axes of the slice: x: 2, y: 2, z: 4, core: 2. Of those that a mesh axis runs over, the one named last changes fastest.
Arguments:
- features: float32 [8, 768, 1024], P(None, ('crow', 'ccol'), 'seq'), may hold values from -6 to 6
- first_channel_scale: float32 [768], P(('crow', 'ccol')), may hold values from 0.5 to 2
- first_channel_shift: float32 [768], P(('crow', 'ccol')), may hold values from -3 to 3
- first_conv_bias: float32 [768], P(('crow', 'ccol')), may hold values from -3 to 3
- first_kernel_taps: float32 [5, 768, 768], P(None, ('crow', 'ccol')), may hold values from -0.09375 to 0.09375
- second_channel_scale: float32 [768], P(('crow', 'ccol')), may hold values from 0.5 to 2
- second_channel_shift: float32 [768], P(('crow', 'ccol')), may hold values from -3 to 3
- second_conv_bias: float32 [768], P(('crow', 'ccol')), may hold values from -3 to 3
- second_kernel_taps: float32 [5, 768, 768], P(None, ('crow', 'ccol')), may hold values from -0.09375 to 0.09375
- up_weight: float32 [1536, 768], P(('crow', 'ccol')), may hold values from -0.21875 to 0.21875
- norm_gain: float32 [1536], replicated, may hold values from 0.5 to 2
- qkv_weight: float32 [1536, 4608], P(None, ('crow', 'ccol')), as said below
- out_weight: float32 [1536, 1536], P(('crow', 'ccol')), may hold values from -0.625 to 0.625
Outputs:
- tower_skip_output: float32 [8, 768, 1024], P(None, ('crow', 'ccol'), 'seq')
- attended: float32 [8, 128, 1536], P(None, 'seq', ('crow', 'ccol'))
Inputs may be any that keep to these rules, and one draw needn't show every extreme that they name: `qkv_weight`: entries are of order 1 / sqrt(1536) times a few.
All inputs are finite; a program needn't handle non-finite values.
Results may differ from a plain program's by a relative error of at most 0.0003.
Values sent between devices are 32-bit elements; how exact they have to be, the bound alone decides.
No kernel may reach another device: no remote copies, remote signals or barrier semaphores. Data moves between devices by JAX's collectives and lax.ppermute only.
A program may use at most 192 MiB of HBM per device.

v0:
```python
import math

import jax
import jax.numpy as jnp
from jax import lax
from jax.sharding import PartitionSpec as P

FIRST_DILATION = 2
SECOND_DILATION = 4
POOL = 8
TAPS = 5

MATMUL_PRECISION = lax.Precision.HIGH
CHANNELS = ("crow", "ccol")


def gathered(x, axis_name):
    count = lax.axis_size(axis_name)
    copies = jnp.broadcast_to(x[None], (count,) + x.shape)
    return lax.all_to_all(copies, axis_name, 0, 0, tiled=True)


def summed_scatter(x, axis_name):
    return jnp.sum(lax.all_to_all(x, axis_name, 0, 0, tiled=True), axis=0)


def swap_ccol(x):
    return lax.ppermute(x, "ccol", [(0, 1), (1, 0)])


def shifted_in(edge, forward):
    count = lax.axis_size("seq")
    if forward:
        pairs = [(i, i + 1) for i in range(count - 1)]
    else:
        pairs = [(i + 1, i) for i in range(count - 1)]
    return lax.ppermute(edge, "seq", pairs)


def convolution_block(inputs, bn_scale, bn_shift, conv_bias, kernel, dilation):
    activated = jax.nn.gelu(inputs * bn_scale[:, None] + bn_shift[:, None], approximate=False)
    by_row = gathered(activated, "crow")
    other_core = swap_ccol(by_row)
    core = lax.axis_index("ccol")
    tap_count, out_count, in_count = kernel.shape
    row_count, batch_count, block, rows = by_row.shape
    slot = lax.broadcasted_iota(jnp.int32, (1, 2, 1, 1, 1), 1)
    ordered = jnp.where(slot == core, by_row[:, None], other_core[:, None])
    ordered = jnp.transpose(ordered, (2, 4, 0, 1, 3)).reshape(batch_count, rows, in_count)
    products = jnp.einsum("btc,koc->kbto", ordered, kernel, precision=MATMUL_PRECISION)
    batch_count, rows = inputs.shape[0], inputs.shape[2]
    width = 2 * dilation
    padded = jnp.pad(products, ((0, 0), (0, 0), (2 * width, 2 * width), (0, 0)))
    spread = None
    for tap_index in range(tap_count):
        offset = tap_index * dilation
        term = padded[tap_index, :, offset : offset + rows + 2 * width, :]
        spread = term if spread is None else spread + term
    spread = jnp.swapaxes(spread, 1, 2)
    to_left = jnp.swapaxes(spread[..., :width], 1, 2)
    to_right = jnp.swapaxes(spread[..., rows + width :], 1, 2)
    from_left = jnp.swapaxes(shifted_in(to_right, True), 1, 2)
    from_right = jnp.swapaxes(shifted_in(to_left, False), 1, 2)
    edges = jnp.concatenate(
        [from_left, jnp.zeros((batch_count, out_count, rows - 2 * width), jnp.float32), from_right],
        axis=2,
    )
    summed = spread[..., width : width + rows] + edges
    return inputs + summed + conv_bias[:, None]


def rotate(values, positions):
    half_width = values.shape[-1] // 2
    frequency = jnp.exp(
        -math.log(10000.0) * jnp.arange(half_width).astype(jnp.float32) / half_width
    )
    angle = positions[:, None] * frequency[None, :]
    cosine = jnp.cos(angle)
    sine_part = jnp.sin(angle)
    lower_half = values[..., :half_width]
    upper_half = values[..., half_width:]
    return jnp.concatenate(
        [
            lower_half * cosine - upper_half * sine_part,
            lower_half * sine_part + upper_half * cosine,
        ],
        axis=-1,
    )


LANES = 128


def packed(x):
    rows, width = x.shape[-2:]
    if (rows * width) % LANES:
        return x
    return x.reshape(x.shape[:-2] + (rows * width // LANES, LANES))


def unpacked(x, rows, width):
    return x.reshape(x.shape[:-2] + (rows, width))


def gathered_packed(x, axis_name):
    rows, width = x.shape[-2:]
    return unpacked(gathered(packed(x), axis_name), rows, width)


def head_attention(hidden_all, norm_gain, qkv_weight, positions):
    group = hidden_all.shape[0]
    attn_width = norm_gain.shape[0]
    squares = jnp.sum(hidden_all * hidden_all, axis=(0, 3))
    gain_blocks = norm_gain.reshape(group, 1, 1, attn_width // group)
    qkv_blocks = qkv_weight.reshape(group, attn_width // group, qkv_weight.shape[1])
    projected = jnp.einsum(
        "nbtj,njo->bto", hidden_all * gain_blocks, qkv_blocks, precision=MATMUL_PRECISION
    )
    root_mean = jnp.sqrt(squares / attn_width + 1e-06)
    projected = projected / root_mean[..., None]
    head_extent = qkv_weight.shape[1] // 3
    query_rows = rotate(projected[..., :head_extent], positions) / math.sqrt(head_extent)
    key_matrix = rotate(projected[..., head_extent : 2 * head_extent], positions)
    return query_rows, key_matrix, projected[..., 2 * head_extent :]


def attention_by_batch(pooled, up_weight, norm_gain, qkv_weight, out_weight):
    batch_count, pooled_rows, channels = pooled.shape
    seq = lax.axis_size("seq")
    group = lax.axis_size(CHANNELS)
    per = batch_count // seq
    length = seq * pooled_rows
    mine = lax.all_to_all(pooled.reshape(seq, per, pooled_rows, channels), "seq", 0, 0, tiled=True)
    mine = jnp.transpose(mine, (1, 0, 2, 3)).reshape(per, length, channels)
    pooled_all = gathered_packed(mine, CHANNELS)
    up_blocks = up_weight.reshape(up_weight.shape[0], group, channels)
    hidden = jnp.einsum("nbti,oni->bto", pooled_all, up_blocks, precision=MATMUL_PRECISION)
    hidden_all = gathered_packed(hidden, CHANNELS)
    positions = jnp.arange(length, dtype=jnp.int32).astype(jnp.float32)
    query_rows, key_matrix, value_matrix = head_attention(hidden_all, norm_gain, qkv_weight, positions)
    attention_scores = jnp.einsum(
        "btc,bxc->btx", query_rows, key_matrix, precision=MATMUL_PRECISION
    )
    top = jnp.max(attention_scores, axis=2)
    probabilities = jnp.exp(attention_scores - top[..., None])
    denominator = jnp.sum(probabilities, axis=2)
    weighted_values = jnp.einsum(
        "btx,bxe->bte", probabilities, value_matrix, precision=MATMUL_PRECISION
    )
    head_result = weighted_values / denominator[..., None]
    out_width = out_weight.shape[1] // group
    out_blocks = out_weight.reshape(out_weight.shape[0], group, out_width)
    shares = jnp.einsum("btd,dne->nbte", head_result, out_blocks, precision=MATMUL_PRECISION)
    summed = jnp.sum(lax.all_to_all(packed(shares), CHANNELS, 0, 0, tiled=True), axis=0)
    summed = unpacked(summed, length, out_width)
    by_block = jnp.transpose(summed.reshape(per, seq, pooled_rows, out_width), (1, 0, 2, 3))
    back = lax.all_to_all(packed(by_block), "seq", 0, 0, tiled=True)
    return unpacked(back, pooled_rows, out_width).reshape(batch_count, pooled_rows, out_width)


def attention_by_position(pooled, up_weight, norm_gain, qkv_weight, out_weight):
    batch_count, pooled_rows, channels = pooled.shape
    group = lax.axis_size(CHANNELS)
    pooled_all = gathered_packed(pooled, CHANNELS)
    up_blocks = up_weight.reshape(up_weight.shape[0], group, channels)
    hidden = jnp.einsum("nbti,oni->bto", pooled_all, up_blocks, precision=MATMUL_PRECISION)
    hidden_all = gathered_packed(hidden, CHANNELS)
    positions = (
        lax.axis_index("seq") * pooled_rows + jnp.arange(pooled_rows, dtype=jnp.int32)
    ).astype(jnp.float32)
    query_rows, key_matrix, value_matrix = head_attention(hidden_all, norm_gain, qkv_weight, positions)
    head_extent = query_rows.shape[-1]
    keys_and_values = jnp.concatenate([key_matrix, value_matrix], axis=2)
    kv_all = gathered(keys_and_values, "seq")
    attention_scores = jnp.einsum(
        "btc,nbxc->btnx", query_rows, kv_all[..., :head_extent], precision=MATMUL_PRECISION
    )
    top = jnp.max(attention_scores, axis=(2, 3))
    probabilities = jnp.exp(attention_scores - top[..., None, None])
    denominator = jnp.sum(probabilities, axis=(2, 3))
    weighted_values = jnp.einsum(
        "btnx,nbxe->bte", probabilities, kv_all[..., head_extent:], precision=MATMUL_PRECISION
    )
    head_result = weighted_values / denominator[..., None]
    out_width = out_weight.shape[1] // group
    out_blocks = out_weight.reshape(out_weight.shape[0], group, out_width)
    shares = jnp.einsum("btd,dne->nbte", head_result, out_blocks, precision=MATMUL_PRECISION)
    summed = jnp.sum(lax.all_to_all(packed(shares), CHANNELS, 0, 0, tiled=True), axis=0)
    return unpacked(summed, pooled_rows, out_width)


def per_device(
    features,
    first_channel_scale,
    first_channel_shift,
    first_conv_bias,
    first_kernel_taps,
    second_channel_scale,
    second_channel_shift,
    second_conv_bias,
    second_kernel_taps,
    up_weight,
    norm_gain,
    qkv_weight,
    out_weight,
):
    batch_count = features.shape[0]
    channels = features.shape[1]
    row_count = features.shape[2]
    first_part = convolution_block(
        features,
        first_channel_scale,
        first_channel_shift,
        first_conv_bias,
        first_kernel_taps,
        FIRST_DILATION,
    )
    tower_skip_output = convolution_block(
        first_part,
        second_channel_scale,
        second_channel_shift,
        second_conv_bias,
        second_kernel_taps,
        SECOND_DILATION,
    )
    pooled_rows = row_count // POOL
    pooled = jnp.transpose(
        jnp.max(tower_skip_output.reshape(batch_count, channels, pooled_rows, POOL), axis=3),
        (0, 2, 1),
    )
    if batch_count % lax.axis_size("seq") == 0:
        attended = attention_by_batch(pooled, up_weight, norm_gain, qkv_weight, out_weight)
    else:
        attended = attention_by_position(pooled, up_weight, norm_gain, qkv_weight, out_weight)
    return (tower_skip_output, attended)


def solution(mesh):
    placed = (
        P(None, CHANNELS, "seq"),
        P(CHANNELS),
        P(CHANNELS),
        P(CHANNELS),
        P(None, CHANNELS, None),
        P(CHANNELS),
        P(CHANNELS),
        P(CHANNELS),
        P(None, CHANNELS, None),
        P(CHANNELS, None),
        P(),
        P(None, CHANNELS),
        P(CHANNELS, None),
    )
    return jax.shard_map(
        per_device,
        mesh=mesh,
        in_specs=placed,
        out_specs=(P(None, CHANNELS, "seq"), P(None, "seq", CHANNELS)),
        check_vma=False,
    )
```

profile of v0, /device:TPU:0, one launch (start us, length us, event | category | flops | bytes accessed | tf_op | source)
XLA Modules:
  0.0 254.4 jit_solution(8109943709931020399)
XLA Ops:
  0.6 3.0 %fusion.36 = f32[8,96,256]{2,1,0:T(8,128)S(1)} fusion(f32[8,96,256]{2,1,0:T(8,128)} %param.13, f32[96]{0:T(128)} %param.15, f32[96]{0:T(128)} %param.14), kind=kLoop, calls=%fused_computation.47 | loop fusion | flops 12976128 | bytes 1573632 | tf_op jit(solution)/shard_map/mul | solution.py:41
  4.1 41.7 %all_to_all.35 = f32[4,8,96,256]{3,2,1,0:T(8,128)} all-to-all(f32[4,8,96,256]{3,2,1,0:T(8,128)S(1)} %broadcast_in_dim.111), channel_id=1, replica_groups=mesh['seq'=4,'crow'=4,'ccol'=2] {'crow'}, dimensions={0} | all-to-all | bytes 6291456 | tf_op jit(solution)/shard_map/all_to_all | solution.py:20
  45.9 5.8 %collective-permute-done = f32[4,8,96,256]{3,2,1,0:T(8,128)} collective-permute-done((f32[4,8,96,256]{3,2,1,0:T(8,128)}, f32[4,8,96,256]{3,2,1,0:T(8,128)}, u32[]{:S(2)}, u32[]{:S(2)}) %collective-permute-start) | collective-permute-done | bytes 3145760 | tf_op jit(solution)/shard_map/ppermute | solution.py:28
  51.8 3.8 %bitcast_select_fusion.1 = f32[8,256,768]{1,2,0:T(8,128)S(1)} fusion(pred[768]{0:T(1024)(128)(4,1)S(1)} %broadcast_in_dim.109, f32[4,8,96,256]{3,2,1,0:T(8,128)} %all_to_all.35, f32[4,8,96,256]{3,2,1,0:T(8,128)} %collective-permute-done), kind=kLoop, calls=%fused_computation.16 | loop fusion | flops 1572864 | bytes 12583680 | tf_op jit(solution)/shard_map/jit(_where)/select_n | solution.py:48
  55.5 5.4 %fusion.10 = f32[5,8,256,96]{2,3,0,1:T(8,128)S(1)} fusion(f32[8,256,768]{1,2,0:T(8,128)S(1)} %bitcast_select_fusion.1, f32[5,96,768]{2,1,0:T(8,128)S(1)} %copy-done), kind=kOutput, calls=%fused_computation.20 | convolution fusion | flops 4529848320 | bytes 11698176 | tf_op jit(solution)/shard_map/btc,koc->kbto/dot_general | solution.py:50
  61.0 1.3 fusion.25
  62.4 1.3 collective-permute-start.2
  63.7 4.8 %collective-permute-start.1 = (f32[8,4,96]{1,2,0:T(8,128)S(1)}, f32[8,4,96]{1,2,0:T(8,128)S(1)}, u32[]{:S(2)}, u32[]{:S(2)}) collective-permute-start(f32[8,4,96]{1,2,0:T(8,128)S(1)} %get-tuple-element.6), channel_id=1, source_target_pairs={{0,8},{8,16},{16,24},{1,9},{9,17},{17,25},{2,10},{10,18},{18,26},{... | collective-permute-start | bytes 36872 | tf_op jit(solution)/shard_map/ppermute | solution.py:37
  68.6 6.9 %collective-permute-done.2 = f32[8,4,96]{1,2,0:T(8,128)S(1)} collective-permute-done((f32[8,4,96]{1,2,0:T(8,128)S(1)}, f32[8,4,96]{1,2,0:T(8,128)S(1)}, u32[]{:S(2)}, u32[]{:S(2)}) %collective-permute-start.2) | collective-permute-done | bytes 12320 | tf_op jit(solution)/shard_map/ppermute | solution.py:37
  76.7 2.0 fusion.38
  79.1 38.6 %all_to_all.36 = f32[4,8,96,256]{3,2,1,0:T(8,128)S(1)} all-to-all(f32[4,8,96,256]{3,2,1,0:T(8,128)S(1)} %broadcast_in_dim.119), channel_id=1, replica_groups=mesh['seq'=4,'crow'=4,'ccol'=2] {'crow'}, dimensions={0} | all-to-all | bytes 6291456 | tf_op jit(solution)/shard_map/all_to_all | solution.py:20
  117.6 5.7 %collective-permute-done.3 = f32[4,8,96,256]{3,2,1,0:T(8,128)S(1)} collective-permute-done((f32[4,8,96,256]{3,2,1,0:T(8,128)S(1)}, f32[4,8,96,256]{3,2,1,0:T(8,128)S(1)}, u32[]{:S(2)}, u32[]{:S(2)}) %collective-permute-start.3) | collective-permute-done | bytes 3145760 | tf_op jit(solution)/shard_map/ppermute | solution.py:28
  124.2 5.4 %fusion.7 = f32[5,8,256,96]{2,3,1,0:T(8,128)S(1)} fusion(f32[8,256,768]{1,2,0:T(8,128)S(1)} %bitcast_select_fusion, f32[5,96,768]{2,1,0:T(8,128)S(1)} %copy-done.5), kind=kOutput, calls=%fused_computation.19 | convolution fusion | flops 4529848320 | bytes 11698176 | tf_op jit(solution)/shard_map/btc,koc->kbto/dot_general | solution.py:50
  129.6 1.3 fusion.30
  131.1 1.3 collective-permute-start.5
  132.4 5.0 %collective-permute-start.4 = (f32[8,8,96]{1,2,0:T(8,128)S(1)}, f32[8,8,96]{1,2,0:T(8,128)S(1)}, u32[]{:S(2)}, u32[]{:S(2)}) collective-permute-start(f32[8,8,96]{1,2,0:T(8,128)S(1)} %get-tuple-element.4), channel_id=1, source_target_pairs={{0,8},{8,16},{16,24},{1,9},{9,17},{17,25},{2,10},{10,18},{18,26},{... | collective-permute-start | bytes 73736 | tf_op jit(solution)/shard_map/ppermute | solution.py:37
  137.5 7.4 %collective-permute-done.5 = f32[8,8,96]{1,2,0:T(8,128)S(1)} collective-permute-done((f32[8,8,96]{1,2,0:T(8,128)S(1)}, f32[8,8,96]{1,2,0:T(8,128)S(1)}, u32[]{:S(2)}, u32[]{:S(2)}) %collective-permute-start.5) | collective-permute-done | bytes 24608 | tf_op jit(solution)/shard_map/ppermute | solution.py:37
  147.1 11.7 %all_to_all.37 = f32[4,2,32,96]{3,2,1,0:T(8,128)S(1)} all-to-all(f32[4,2,32,96]{3,2,1,0:T(8,128)S(1)} %bitcast.120), channel_id=1, replica_groups=mesh['seq'=4,'crow'=4,'ccol'=2] {'seq'}, dimensions={0} | all-to-all | bytes 196608 | tf_op jit(solution)/shard_map/all_to_all | solution.py:133
  159.9 3.8 %all-to-all-start.3 = ((f32[8,2,96,128]{3,2,1,0:T(8,128)}), f32[8,2,96,128]{3,2,1,0:T(8,128)S(1)}, u32[]{:S(2)}, u32[]{:S(2)}) async-start(f32[8,2,96,128]{3,2,1,0:T(8,128)} %broadcast_in_dim.128), calls=%async_computation.3 | async-start | bytes 1572864 | tf_op jit(solution)/shard_map/all_to_all | solution.py:20
  163.7 1.4 reshape.144
  165.1 10.9 %all-to-all-done.3 = f32[8,2,96,128]{3,2,1,0:T(8,128)S(1)} async-done(((f32[8,2,96,128]{3,2,1,0:T(8,128)}), f32[8,2,96,128]{3,2,1,0:T(8,128)S(1)}, u32[]{:S(2)}, u32[]{:S(2)}) %all-to-all-start.3) | async-done | bytes 786464 | tf_op jit(solution)/shard_map/all_to_all | solution.py:20
  177.2 1.3 broadcast_in_dim.130
  178.5 3.6 %all-to-all-start.4 = ((f32[8,2,192,128]{3,2,1,0:T(8,128)}), f32[8,2,192,128]{3,2,1,0:T(8,128)S(1)}, u32[]{:S(2)}, u32[]{:S(2)}) async-start(f32[8,2,192,128]{3,2,1,0:T(8,128)} %broadcast_in_dim.130), calls=%async_computation.4 | async-start | bytes 3145728 | tf_op jit(solution)/shard_map/all_to_all | solution.py:20
  182.1 5.4 %copy.57 = f32[1536,576]{1,0:T(8,128)} copy(f32[1536,576]{0,1:T(8,128)} %param.24) | data formatting | bytes 7077888 | tf_op args[11]
  187.6 1.6 copy.79
  189.5 13.6 %all-to-all-done.4 = f32[8,2,192,128]{3,2,1,0:T(8,128)S(1)} async-done(((f32[8,2,192,128]{3,2,1,0:T(8,128)}), f32[8,2,192,128]{3,2,1,0:T(8,128)S(1)}, u32[]{:S(2)}, u32[]{:S(2)}) %all-to-all-start.4) | async-done | bytes 1572896 | tf_op jit(solution)/shard_map/all_to_all | solution.py:20
  203.4 1.8 reshape.145
  205.2 6.9 %fusion.18 = f32[2,128,576]{1,2,0:T(8,128)S(1)} fusion(f32[8,192,576,1]{2,1,3,0:T(8,128)} %bitcast.116, f32[8,2,128,192]{3,2,1,0:T(8,128)} %reshape.145, f32[8,192]{1,0:T(8,128)S(1)} %mul.194, f32[2,128]{1,0:T(2,128)S(1)} %add_sqrt_fusion), kind=kOutput, calls=%fused_computation.26 | convolution fusion | flops 1359495168 | bytes 5708800 | tf_op jit(solution)/shard_map/nbtj,njo->bto/dot_general | solution.py:116
  213.9 1.8 copy.61
  215.7 3.4 %reshape.148 = f32[8,2,192,128]{3,2,1,0:T(8,128)} reshape(f32[8,2,128,192]{3,2,1,0:T(8,128)} %copy.61) | data formatting | bytes 3145728 | tf_op jit(solution)/shard_map/reshape | solution.py:98
  219.1 24.5 %all_to_all.38 = f32[8,2,192,128]{3,2,1,0:T(8,128)S(1)} all-to-all(f32[8,2,192,128]{3,2,1,0:T(8,128)} %reshape.148), channel_id=1, replica_groups=mesh['seq'=4,'crow'=4,'ccol'=2] {'crow','ccol'}, dimensions={0} | all-to-all | bytes 3145728 | tf_op jit(solution)/shard_map/all_to_all | solution.py:154
  243.9 9.7 %all_to_all.39 = f32[4,2,48,128]{3,2,1,0:T(8,128)S(1)} all-to-all(f32[4,2,48,128]{3,2,1,0:T(8,128)S(1)} %copy.62), channel_id=1, replica_groups=mesh['seq'=4,'crow'=4,'ccol'=2] {'seq'}, dimensions={0} | all-to-all | bytes 393216 | tf_op jit(solution)/shard_map/all_to_all | solution.py:157
  (67 shorter events, 11.5 us)
Async XLA Ops:
  0.6 54.9 %copy-start = (f32[5,96,768]{2,1,0:T(8,128)S(1)}, f32[5,96,768]{2,1,0:T(8,128)}, u32[]{:S(2)}) copy-start(f32[5,96,768]{2,1,0:T(8,128)} %param.17) | copy-start | bytes 4423684
  45.8 6.0 %collective-permute-start = (f32[4,8,96,256]{3,2,1,0:T(8,128)}, f32[4,8,96,256]{3,2,1,0:T(8,128)}, u32[]{:S(2)}, u32[]{:S(2)}) collective-permute-start(f32[4,8,96,256]{3,2,1,0:T(8,128)} %all_to_all.35), channel_id=1, source_target_pairs={{0,1},{1,0},{2,3},{3,2},{4,5},{5,4},{6,7},{7,6},{8,9},{9,8},{10,11... | collective-permute-start | bytes 9437192 | tf_op jit(solution)/shard_map/ppermute | solution.py:28
  60.9 15.7 %copy-start.4 = (f32[8,96,256]{2,1,0:T(8,128)S(1)}, f32[8,96,256]{2,1,0:T(8,128)}, u32[]{:S(2)}) copy-start(f32[8,96,256]{2,1,0:T(8,128)} %param.13) | copy-start | bytes 2359300
  61.0 15.7 %copy-start.9 = (f32[96]{0:T(128)S(1)}, f32[96]{0:T(128)}, u32[]{:S(2)}) copy-start(f32[96]{0:T(128)} %param.19) | copy-start | bytes 1156
  61.0 15.7 %copy-start.10 = (f32[96]{0:T(128)S(1)}, f32[96]{0:T(128)}, u32[]{:S(2)}) copy-start(f32[96]{0:T(128)} %param.18) | copy-start | bytes 1156
  61.0 15.7 %copy-start.11 = (f32[96]{0:T(128)S(1)}, f32[96]{0:T(128)}, u32[]{:S(2)}) copy-start(f32[96]{0:T(128)} %param.16) | copy-start | bytes 1156
  62.4 13.0 %collective-permute-start.2 = (f32[8,4,96]{1,2,0:T(8,128)S(1)}, f32[8,4,96]{1,2,0:T(8,128)S(1)}, u32[]{:S(2)}, u32[]{:S(2)}) collective-permute-start(f32[8,4,96]{1,2,0:T(8,128)S(1)} %get-tuple-element.7), channel_id=1, source_target_pairs={{8,0},{16,8},{24,16},{9,1},{17,9},{25,17},{10,2},{18,10},{26,18},{... | collective-permute-start | bytes 36872 | tf_op jit(solution)/shard_map/ppermute | solution.py:37
  63.7 12.9 %collective-permute-start.1 = (f32[8,4,96]{1,2,0:T(8,128)S(1)}, f32[8,4,96]{1,2,0:T(8,128)S(1)}, u32[]{:S(2)}, u32[]{:S(2)}) collective-permute-start(f32[8,4,96]{1,2,0:T(8,128)S(1)} %get-tuple-element.6), channel_id=1, source_target_pairs={{0,8},{8,16},{16,24},{1,9},{9,17},{17,25},{2,10},{10,18},{18,26},{... | collective-permute-start | bytes 36872 | tf_op jit(solution)/shard_map/ppermute | solution.py:37
  117.6 6.6 %copy-start.5 = (f32[5,96,768]{2,1,0:T(8,128)S(1)}, f32[5,96,768]{2,1,0:T(8,128)}, u32[]{:S(2)}) copy-start(f32[5,96,768]{2,1,0:T(8,128)} %param.21) | copy-start | bytes 4423684
  117.6 5.7 %collective-permute-start.3 = (f32[4,8,96,256]{3,2,1,0:T(8,128)S(1)}, f32[4,8,96,256]{3,2,1,0:T(8,128)S(1)}, u32[]{:S(2)}, u32[]{:S(2)}) collective-permute-start(f32[4,8,96,256]{3,2,1,0:T(8,128)S(1)} %all_to_all.36), channel_id=1, source_target_pairs={{0,1},{1,0},{2,3},{3,2},{4,5},{5,4},{6,7},{7,6},{8,9},{9,8},{10,11... | collective-permute-start | bytes 9437192 | tf_op jit(solution)/shard_map/ppermute | solution.py:28
  129.6 16.4 %copy-start.8 = (f32[96]{0:T(128)S(1)}, f32[96]{0:T(128)}, u32[]{:S(2)}) copy-start(f32[96]{0:T(128)} %param.20) | copy-start | bytes 1156
  131.1 13.8 %collective-permute-start.5 = (f32[8,8,96]{1,2,0:T(8,128)S(1)}, f32[8,8,96]{1,2,0:T(8,128)S(1)}, u32[]{:S(2)}, u32[]{:S(2)}) collective-permute-start(f32[8,8,96]{1,2,0:T(8,128)S(1)} %get-tuple-element.5), channel_id=1, source_target_pairs={{8,0},{16,8},{24,16},{9,1},{17,9},{25,17},{10,2},{18,10},{26,18},{... | collective-permute-start | bytes 73736 | tf_op jit(solution)/shard_map/ppermute | solution.py:37
  132.4 13.7 %collective-permute-start.4 = (f32[8,8,96]{1,2,0:T(8,128)S(1)}, f32[8,8,96]{1,2,0:T(8,128)S(1)}, u32[]{:S(2)}, u32[]{:S(2)}) collective-permute-start(f32[8,8,96]{1,2,0:T(8,128)S(1)} %get-tuple-element.4), channel_id=1, source_target_pairs={{0,8},{8,16},{16,24},{1,9},{9,17},{17,25},{2,10},{10,18},{18,26},{... | collective-permute-start | bytes 73736 | tf_op jit(solution)/shard_map/ppermute | solution.py:37
  146.5 13.4 %copy-start.3 = (f32[8,96,256]{2,1,0:T(8,128)}, f32[8,96,256]{2,1,0:T(8,128)S(1)}, u32[]{:S(2)}) copy-start(f32[8,96,256]{2,1,0:T(8,128)S(1)} %fusion.40) | copy-start | bytes 2359300
  159.9 16.1 %all-to-all-start.3 = ((f32[8,2,96,128]{3,2,1,0:T(8,128)}), f32[8,2,96,128]{3,2,1,0:T(8,128)S(1)}, u32[]{:S(2)}, u32[]{:S(2)}) async-start(f32[8,2,96,128]{3,2,1,0:T(8,128)} %broadcast_in_dim.128), calls=%async_computation.3 | async-start | bytes 1572864 | tf_op jit(solution)/shard_map/all_to_all | solution.py:20
  178.5 24.5 %all-to-all-start.4 = ((f32[8,2,192,128]{3,2,1,0:T(8,128)}), f32[8,2,192,128]{3,2,1,0:T(8,128)S(1)}, u32[]{:S(2)}, u32[]{:S(2)}) async-start(f32[8,2,192,128]{3,2,1,0:T(8,128)} %broadcast_in_dim.130), calls=%async_computation.4 | async-start | bytes 3145728 | tf_op jit(solution)/shard_map/all_to_all | solution.py:20
  182.1 5.4 %copy-start.7 = (f32[1536]{0:T(1024)S(1)}, f32[1536]{0:T(1024)}, u32[]{:S(2)}) copy-start(f32[1536]{0:T(1024)} %param.23) | copy-start | bytes 18436
  182.1 5.5 %copy-start.6 = (f32[192,1536]{1,0:T(8,128)S(1)}, f32[192,1536]{1,0:T(8,128)}, u32[]{:S(2)}) copy-start(f32[192,1536]{1,0:T(8,128)} %param.25) | copy-start | bytes 3538948
  205.2 7.8 %copy-start.2 = (f32[192,1536]{0,1:T(8,128)S(1)}, f32[192,1536]{0,1:T(8,128)}, u32[]{:S(2)}) copy-start(f32[192,1536]{0,1:T(8,128)} %copy.79) | copy-start | bytes 3538948
  215.7 38.7 %copy-start.1 = (f32[5,96,768]{2,1,0:T(8,128)S(1)}, f32[5,96,768]{2,1,0:T(8,128)}, u32[]{:S(2)}) copy-start(f32[5,96,768]{2,1,0:T(8,128)} %param.17) | copy-start | bytes 4423684
where the time goes:
time: 255 us; the launch traced here: 254 us
  blocking collectives  126 us (49%)
  waiting for transfers between devices  52.6 us (21%)
  local copies, waits for them, and re-layouts  21.3 us (8%)
  matrix products  19.9 us (8%)
  starting transfers between devices  19.7 us (8%)
  other arithmetic  13.7 us (5%)
    all_to_all x2, blocking collectives, gathered(): return lax.all_to_all(copies, axis_name, 0, 0, tiled=True)  80.2 us
    all_to_all x1, blocking collectives, attention_by_batch(): lax.all_to_all(packed(shares), CHANNELS, 0, 0, tiled=True)  24.5 us
    all_to_all x2, waiting for transfers between devices, gathered(): return lax.all_to_all(copies, axis_name, 0, 0, tiled=True)  24.5 us
    ppermute x4, waiting for transfers between devices, shifted_in(): return lax.ppermute(edge, 'seq', pairs)  16.6 us
    ppermute x4, starting transfers between devices, shifted_in(): return lax.ppermute(edge, 'seq', pairs)  12.4 us
    all_to_all x1, blocking collectives, attention_by_batch(): lax.all_to_all(pooled.reshape(seq, per, pooled_rows, channels), 'seq', 0,...  11.7 us
    ppermute x2, waiting for transfers between devices, swap_ccol(): return lax.ppermute(x, 'ccol', [(0, 1), (1, 0)])  11.5 us
    dot_general x2, matrix products, convolution_block(): jnp.einsum('btc,koc->kbto', ordered, kernel, precision=MATMUL_PRECISION)  10.8 us
  transfers between devices with their start and end apart: 8, of which 8 were waited for; matrix products, arithmetic and copies ran while one was open for 4% of the time, Pallas kernels for 0%

commit v1 on v0

--- a/solution.py
+++ b/solution.py
@@ -151,8 +151,7 @@
     out_width = out_weight.shape[1] // group
     out_blocks = out_weight.reshape(out_weight.shape[0], group, out_width)
     shares = jnp.einsum("btd,dne->nbte", head_result, out_blocks, precision=MATMUL_PRECISION)
-    summed = jnp.sum(lax.all_to_all(packed(shares), CHANNELS, 0, 0, tiled=True), axis=0)
-    summed = unpacked(summed, length, out_width)
+    summed = jnp.sum(lax.all_to_all(shares, CHANNELS, 0, 0, tiled=True), axis=0)
     by_block = jnp.transpose(summed.reshape(per, seq, pooled_rows, out_width), (1, 0, 2, 3))
     back = lax.all_to_all(packed(by_block), "seq", 0, 0, tiled=True)
     return unpacked(back, pooled_rows, out_width).reshape(batch_count, pooled_rows, out_width)

time: 255 us -> 249 us (0.976)
  local copies, waits for them, and re-layouts: 21.3 us -> 16.3 us
    reshape x3 -> x2, local copies, waits for them, and re-layouts: 3.52 us -> 0.16 us  [packed(): return x.reshape(x.shape[:-2] + (rows * width // LANES, LANES))]
where the time goes in v1:
time: 249 us; the launch traced here: 248 us
  blocking collectives  125 us (50%)
  waiting for transfers between devices  52.6 us (21%)
  matrix products  19.9 us (8%)
  starting transfers between devices  19.7 us (8%)
  local copies, waits for them, and re-layouts  16.3 us (7%)
  other arithmetic  13.7 us (6%)
    all_to_all x2, blocking collectives, gathered(): return lax.all_to_all(copies, axis_name, 0, 0, tiled=True)  80.2 us
    all_to_all x2, waiting for transfers between devices, gathered(): return lax.all_to_all(copies, axis_name, 0, 0, tiled=True)  24.5 us
    all_to_all x1, blocking collectives, attention_by_batch(): summed = jnp.sum(lax.all_to_all(shares, CHANNELS, 0, 0, tiled=True), axis=0)  23.5 us
    ppermute x4, waiting for transfers between devices, shifted_in(): return lax.ppermute(edge, 'seq', pairs)  16.6 us
    ppermute x4, starting transfers between devices, shifted_in(): return lax.ppermute(edge, 'seq', pairs)  12.4 us
    all_to_all x1, blocking collectives, attention_by_batch(): lax.all_to_all(pooled.reshape(seq, per, pooled_rows, channels), 'seq', 0,...  11.7 us
    ppermute x2, waiting for transfers between devices, swap_ccol(): return lax.ppermute(x, 'ccol', [(0, 1), (1, 0)])  11.5 us
    dot_general x2, matrix products, convolution_block(): jnp.einsum('btc,koc->kbto', ordered, kernel, precision=MATMUL_PRECISION)  10.8 us
  transfers between devices with their start and end apart: 8, of which 8 were waited for; matrix products, arithmetic and copies ran while one was open for 4% of the time, Pallas kernels for 0%

profile of v1, /device:TPU:0, one launch (start us, length us, event | category | flops | bytes accessed | tf_op | source)
XLA Modules:
  0.0 248.4 jit_solution(9220078337620291212)
XLA Ops:
  0.6 3.0 %fusion.36 = f32[8,96,256]{2,1,0:T(8,128)S(1)} fusion(f32[8,96,256]{2,1,0:T(8,128)} %param.13, f32[96]{0:T(128)} %param.15, f32[96]{0:T(128)} %param.14), kind=kLoop, calls=%fused_computation.47 | loop fusion | flops 12976128 | bytes 1573632 | tf_op jit(solution)/shard_map/mul | solution.py:41
  4.1 41.7 %all_to_all.35 = f32[4,8,96,256]{3,2,1,0:T(8,128)} all-to-all(f32[4,8,96,256]{3,2,1,0:T(8,128)S(1)} %broadcast_in_dim.111), channel_id=1, replica_groups=mesh['seq'=4,'crow'=4,'ccol'=2] {'crow'}, dimensions={0} | all-to-all | bytes 6291456 | tf_op jit(solution)/shard_map/all_to_all | solution.py:20
  45.9 5.8 %collective-permute-done = f32[4,8,96,256]{3,2,1,0:T(8,128)} collective-permute-done((f32[4,8,96,256]{3,2,1,0:T(8,128)}, f32[4,8,96,256]{3,2,1,0:T(8,128)}, u32[]{:S(2)}, u32[]{:S(2)}) %collective-permute-start) | collective-permute-done | bytes 3145760 | tf_op jit(solution)/shard_map/ppermute | solution.py:28
  51.8 3.8 %bitcast_select_fusion.1 = f32[8,256,768]{1,2,0:T(8,128)S(1)} fusion(pred[768]{0:T(1024)(128)(4,1)S(1)} %broadcast_in_dim.109, f32[4,8,96,256]{3,2,1,0:T(8,128)} %all_to_all.35, f32[4,8,96,256]{3,2,1,0:T(8,128)} %collective-permute-done), kind=kLoop, calls=%fused_computation.16 | loop fusion | flops 1572864 | bytes 12583680 | tf_op jit(solution)/shard_map/jit(_where)/select_n | solution.py:48
  55.5 5.4 %fusion.10 = f32[5,8,256,96]{2,3,0,1:T(8,128)S(1)} fusion(f32[8,256,768]{1,2,0:T(8,128)S(1)} %bitcast_select_fusion.1, f32[5,96,768]{2,1,0:T(8,128)S(1)} %copy-done), kind=kOutput, calls=%fused_computation.20 | convolution fusion | flops 4529848320 | bytes 11698176 | tf_op jit(solution)/shard_map/btc,koc->kbto/dot_general | solution.py:50
  61.0 1.3 fusion.25
  62.4 1.3 collective-permute-start.2
  63.7 4.8 %collective-permute-start.1 = (f32[8,4,96]{1,2,0:T(8,128)S(1)}, f32[8,4,96]{1,2,0:T(8,128)S(1)}, u32[]{:S(2)}, u32[]{:S(2)}) collective-permute-start(f32[8,4,96]{1,2,0:T(8,128)S(1)} %get-tuple-element.6), channel_id=1, source_target_pairs={{0,8},{8,16},{16,24},{1,9},{9,17},{17,25},{2,10},{10,18},{18,26},{... | collective-permute-start | bytes 36872 | tf_op jit(solution)/shard_map/ppermute | solution.py:37
  68.6 6.9 %collective-permute-done.2 = f32[8,4,96]{1,2,0:T(8,128)S(1)} collective-permute-done((f32[8,4,96]{1,2,0:T(8,128)S(1)}, f32[8,4,96]{1,2,0:T(8,128)S(1)}, u32[]{:S(2)}, u32[]{:S(2)}) %collective-permute-start.2) | collective-permute-done | bytes 12320 | tf_op jit(solution)/shard_map/ppermute | solution.py:37
  75.5 1.2 collective-permute-done.1
  76.7 2.0 fusion.38
  79.1 38.6 %all_to_all.36 = f32[4,8,96,256]{3,2,1,0:T(8,128)S(1)} all-to-all(f32[4,8,96,256]{3,2,1,0:T(8,128)S(1)} %broadcast_in_dim.119), channel_id=1, replica_groups=mesh['seq'=4,'crow'=4,'ccol'=2] {'crow'}, dimensions={0} | all-to-all | bytes 6291456 | tf_op jit(solution)/shard_map/all_to_all | solution.py:20
  117.6 5.7 %collective-permute-done.3 = f32[4,8,96,256]{3,2,1,0:T(8,128)S(1)} collective-permute-done((f32[4,8,96,256]{3,2,1,0:T(8,128)S(1)}, f32[4,8,96,256]{3,2,1,0:T(8,128)S(1)}, u32[]{:S(2)}, u32[]{:S(2)}) %collective-permute-start.3) | collective-permute-done | bytes 3145760 | tf_op jit(solution)/shard_map/ppermute | solution.py:28
  124.2 5.4 %fusion.7 = f32[5,8,256,96]{2,3,1,0:T(8,128)S(1)} fusion(f32[8,256,768]{1,2,0:T(8,128)S(1)} %bitcast_select_fusion, f32[5,96,768]{2,1,0:T(8,128)S(1)} %copy-done.5), kind=kOutput, calls=%fused_computation.19 | convolution fusion | flops 4529848320 | bytes 11698176 | tf_op jit(solution)/shard_map/btc,koc->kbto/dot_general | solution.py:50
  129.6 1.3 fusion.30
  131.1 1.3 collective-permute-start.5
  132.4 5.0 %collective-permute-start.4 = (f32[8,8,96]{1,2,0:T(8,128)S(1)}, f32[8,8,96]{1,2,0:T(8,128)S(1)}, u32[]{:S(2)}, u32[]{:S(2)}) collective-permute-start(f32[8,8,96]{1,2,0:T(8,128)S(1)} %get-tuple-element.4), channel_id=1, source_target_pairs={{0,8},{8,16},{16,24},{1,9},{9,17},{17,25},{2,10},{10,18},{18,26},{... | collective-permute-start | bytes 73736 | tf_op jit(solution)/shard_map/ppermute | solution.py:37
  137.5 7.4 %collective-permute-done.5 = f32[8,8,96]{1,2,0:T(8,128)S(1)} collective-permute-done((f32[8,8,96]{1,2,0:T(8,128)S(1)}, f32[8,8,96]{1,2,0:T(8,128)S(1)}, u32[]{:S(2)}, u32[]{:S(2)}) %collective-permute-start.5) | collective-permute-done | bytes 24608 | tf_op jit(solution)/shard_map/ppermute | solution.py:37
  144.9 1.2 collective-permute-done.4
  147.1 11.7 %all_to_all.37 = f32[4,2,32,96]{3,2,1,0:T(8,128)S(1)} all-to-all(f32[4,2,32,96]{3,2,1,0:T(8,128)S(1)} %bitcast.120), channel_id=1, replica_groups=mesh['seq'=4,'crow'=4,'ccol'=2] {'seq'}, dimensions={0} | all-to-all | bytes 196608 | tf_op jit(solution)/shard_map/all_to_all | solution.py:133
  159.9 3.8 %all-to-all-start.3 = ((f32[8,2,96,128]{3,2,1,0:T(8,128)}), f32[8,2,96,128]{3,2,1,0:T(8,128)S(1)}, u32[]{:S(2)}, u32[]{:S(2)}) async-start(f32[8,2,96,128]{3,2,1,0:T(8,128)} %broadcast_in_dim.128), calls=%async_computation.3 | async-start | bytes 1572864 | tf_op jit(solution)/shard_map/all_to_all | solution.py:20
  163.7 1.4 reshape.144
  165.1 10.9 %all-to-all-done.3 = f32[8,2,96,128]{3,2,1,0:T(8,128)S(1)} async-done(((f32[8,2,96,128]{3,2,1,0:T(8,128)}), f32[8,2,96,128]{3,2,1,0:T(8,128)S(1)}, u32[]{:S(2)}, u32[]{:S(2)}) %all-to-all-start.3) | async-done | bytes 786464 | tf_op jit(solution)/shard_map/all_to_all | solution.py:20
  177.2 1.3 broadcast_in_dim.130
  178.5 3.6 %all-to-all-start.4 = ((f32[8,2,192,128]{3,2,1,0:T(8,128)}), f32[8,2,192,128]{3,2,1,0:T(8,128)S(1)}, u32[]{:S(2)}, u32[]{:S(2)}) async-start(f32[8,2,192,128]{3,2,1,0:T(8,128)} %broadcast_in_dim.130), calls=%async_computation.4 | async-start | bytes 3145728 | tf_op jit(solution)/shard_map/all_to_all | solution.py:20
  182.1 5.4 %copy.55 = f32[1536,576]{1,0:T(8,128)} copy(f32[1536,576]{0,1:T(8,128)} %param.24) | data formatting | bytes 7077888 | tf_op args[11]
  187.6 1.6 copy.79
  189.5 13.6 %all-to-all-done.4 = f32[8,2,192,128]{3,2,1,0:T(8,128)S(1)} async-done(((f32[8,2,192,128]{3,2,1,0:T(8,128)}), f32[8,2,192,128]{3,2,1,0:T(8,128)S(1)}, u32[]{:S(2)}, u32[]{:S(2)}) %all-to-all-start.4) | async-done | bytes 1572896 | tf_op jit(solution)/shard_map/all_to_all | solution.py:20
  203.4 1.8 reshape.145
  205.2 6.9 %fusion.18 = f32[2,128,576]{1,2,0:T(8,128)S(1)} fusion(f32[8,192,576,1]{2,1,3,0:T(8,128)} %bitcast.116, f32[8,2,128,192]{3,2,1,0:T(8,128)} %reshape.145, f32[8,192]{1,0:T(8,128)S(1)} %mul.194, f32[2,128]{1,0:T(2,128)S(1)} %add_sqrt_fusion), kind=kOutput, calls=%fused_computation.26 | convolution fusion | flops 1359495168 | bytes 5708800 | tf_op jit(solution)/shard_map/nbtj,njo->bto/dot_general | solution.py:116
  214.0 23.5 %all_to_all.38 = f32[8,2,128,192]{2,3,1,0:T(8,128)S(1)} all-to-all(f32[8,2,128,192]{2,3,1,0:T(8,128)S(1)} %copy.59), channel_id=1, replica_groups=mesh['seq'=4,'crow'=4,'ccol'=2] {'crow','ccol'}, dimensions={0} | all-to-all | bytes 3145728 | tf_op jit(solution)/shard_map/all_to_all | solution.py:154
  238.0 9.7 %all_to_all.39 = f32[4,2,48,128]{3,2,1,0:T(8,128)S(1)} all-to-all(f32[4,2,48,128]{3,2,1,0:T(8,128)S(1)} %copy.62), channel_id=1, replica_groups=mesh['seq'=4,'crow'=4,'ccol'=2] {'seq'}, dimensions={0} | all-to-all | bytes 393216 | tf_op jit(solution)/shard_map/all_to_all | solution.py:156
  (66 shorter events, 9.3 us)
Async XLA Ops:
  0.6 54.9 %copy-start = (f32[5,96,768]{2,1,0:T(8,128)S(1)}, f32[5,96,768]{2,1,0:T(8,128)}, u32[]{:S(2)}) copy-start(f32[5,96,768]{2,1,0:T(8,128)} %param.17) | copy-start | bytes 4423684
  45.8 6.0 %collective-permute-start = (f32[4,8,96,256]{3,2,1,0:T(8,128)}, f32[4,8,96,256]{3,2,1,0:T(8,128)}, u32[]{:S(2)}, u32[]{:S(2)}) collective-permute-start(f32[4,8,96,256]{3,2,1,0:T(8,128)} %all_to_all.35), channel_id=1, source_target_pairs={{0,1},{1,0},{2,3},{3,2},{4,5},{5,4},{6,7},{7,6},{8,9},{9,8},{10,11... | collective-permute-start | bytes 9437192 | tf_op jit(solution)/shard_map/ppermute | solution.py:28
  60.9 15.7 %copy-start.4 = (f32[8,96,256]{2,1,0:T(8,128)S(1)}, f32[8,96,256]{2,1,0:T(8,128)}, u32[]{:S(2)}) copy-start(f32[8,96,256]{2,1,0:T(8,128)} %param.13) | copy-start | bytes 2359300
  61.0 15.7 %copy-start.9 = (f32[96]{0:T(128)S(1)}, f32[96]{0:T(128)}, u32[]{:S(2)}) copy-start(f32[96]{0:T(128)} %param.19) | copy-start | bytes 1156
  61.0 15.7 %copy-start.10 = (f32[96]{0:T(128)S(1)}, f32[96]{0:T(128)}, u32[]{:S(2)}) copy-start(f32[96]{0:T(128)} %param.18) | copy-start | bytes 1156
  61.0 15.7 %copy-start.11 = (f32[96]{0:T(128)S(1)}, f32[96]{0:T(128)}, u32[]{:S(2)}) copy-start(f32[96]{0:T(128)} %param.16) | copy-start | bytes 1156
  62.4 13.0 %collective-permute-start.2 = (f32[8,4,96]{1,2,0:T(8,128)S(1)}, f32[8,4,96]{1,2,0:T(8,128)S(1)}, u32[]{:S(2)}, u32[]{:S(2)}) collective-permute-start(f32[8,4,96]{1,2,0:T(8,128)S(1)} %get-tuple-element.7), channel_id=1, source_target_pairs={{8,0},{16,8},{24,16},{9,1},{17,9},{25,17},{10,2},{18,10},{26,18},{... | collective-permute-start | bytes 36872 | tf_op jit(solution)/shard_map/ppermute | solution.py:37
  63.7 12.9 %collective-permute-start.1 = (f32[8,4,96]{1,2,0:T(8,128)S(1)}, f32[8,4,96]{1,2,0:T(8,128)S(1)}, u32[]{:S(2)}, u32[]{:S(2)}) collective-permute-start(f32[8,4,96]{1,2,0:T(8,128)S(1)} %get-tuple-element.6), channel_id=1, source_target_pairs={{0,8},{8,16},{16,24},{1,9},{9,17},{17,25},{2,10},{10,18},{18,26},{... | collective-permute-start | bytes 36872 | tf_op jit(solution)/shard_map/ppermute | solution.py:37
  117.6 6.6 %copy-start.5 = (f32[5,96,768]{2,1,0:T(8,128)S(1)}, f32[5,96,768]{2,1,0:T(8,128)}, u32[]{:S(2)}) copy-start(f32[5,96,768]{2,1,0:T(8,128)} %param.21) | copy-start | bytes 4423684
  117.6 5.7 %collective-permute-start.3 = (f32[4,8,96,256]{3,2,1,0:T(8,128)S(1)}, f32[4,8,96,256]{3,2,1,0:T(8,128)S(1)}, u32[]{:S(2)}, u32[]{:S(2)}) collective-permute-start(f32[4,8,96,256]{3,2,1,0:T(8,128)S(1)} %all_to_all.36), channel_id=1, source_target_pairs={{0,1},{1,0},{2,3},{3,2},{4,5},{5,4},{6,7},{7,6},{8,9},{9,8},{10,11... | collective-permute-start | bytes 9437192 | tf_op jit(solution)/shard_map/ppermute | solution.py:28
  129.6 16.4 %copy-start.8 = (f32[96]{0:T(128)S(1)}, f32[96]{0:T(128)}, u32[]{:S(2)}) copy-start(f32[96]{0:T(128)} %param.20) | copy-start | bytes 1156
  131.1 13.8 %collective-permute-start.5 = (f32[8,8,96]{1,2,0:T(8,128)S(1)}, f32[8,8,96]{1,2,0:T(8,128)S(1)}, u32[]{:S(2)}, u32[]{:S(2)}) collective-permute-start(f32[8,8,96]{1,2,0:T(8,128)S(1)} %get-tuple-element.5), channel_id=1, source_target_pairs={{8,0},{16,8},{24,16},{9,1},{17,9},{25,17},{10,2},{18,10},{26,18},{... | collective-permute-start | bytes 73736 | tf_op jit(solution)/shard_map/ppermute | solution.py:37
  132.4 13.7 %collective-permute-start.4 = (f32[8,8,96]{1,2,0:T(8,128)S(1)}, f32[8,8,96]{1,2,0:T(8,128)S(1)}, u32[]{:S(2)}, u32[]{:S(2)}) collective-permute-start(f32[8,8,96]{1,2,0:T(8,128)S(1)} %get-tuple-element.4), channel_id=1, source_target_pairs={{0,8},{8,16},{16,24},{1,9},{9,17},{17,25},{2,10},{10,18},{18,26},{... | collective-permute-start | bytes 73736 | tf_op jit(solution)/shard_map/ppermute | solution.py:37
  146.5 13.4 %copy-start.3 = (f32[8,96,256]{2,1,0:T(8,128)}, f32[8,96,256]{2,1,0:T(8,128)S(1)}, u32[]{:S(2)}) copy-start(f32[8,96,256]{2,1,0:T(8,128)S(1)} %fusion.40) | copy-start | bytes 2359300
  159.9 16.1 %all-to-all-start.3 = ((f32[8,2,96,128]{3,2,1,0:T(8,128)}), f32[8,2,96,128]{3,2,1,0:T(8,128)S(1)}, u32[]{:S(2)}, u32[]{:S(2)}) async-start(f32[8,2,96,128]{3,2,1,0:T(8,128)} %broadcast_in_dim.128), calls=%async_computation.3 | async-start | bytes 1572864 | tf_op jit(solution)/shard_map/all_to_all | solution.py:20
  178.5 24.5 %all-to-all-start.4 = ((f32[8,2,192,128]{3,2,1,0:T(8,128)}), f32[8,2,192,128]{3,2,1,0:T(8,128)S(1)}, u32[]{:S(2)}, u32[]{:S(2)}) async-start(f32[8,2,192,128]{3,2,1,0:T(8,128)} %broadcast_in_dim.130), calls=%async_computation.4 | async-start | bytes 3145728 | tf_op jit(solution)/shard_map/all_to_all | solution.py:20
  182.1 5.4 %copy-start.7 = (f32[1536]{0:T(1024)S(1)}, f32[1536]{0:T(1024)}, u32[]{:S(2)}) copy-start(f32[1536]{0:T(1024)} %param.23) | copy-start | bytes 18436
  182.1 5.5 %copy-start.6 = (f32[192,1536]{1,0:T(8,128)S(1)}, f32[192,1536]{1,0:T(8,128)}, u32[]{:S(2)}) copy-start(f32[192,1536]{1,0:T(8,128)} %param.25) | copy-start | bytes 3538948
  205.2 7.8 %copy-start.2 = (f32[192,1536]{0,1:T(8,128)S(1)}, f32[192,1536]{0,1:T(8,128)}, u32[]{:S(2)}) copy-start(f32[192,1536]{0,1:T(8,128)} %copy.79) | copy-start | bytes 3538948
  213.9 34.6 %copy-start.1 = (f32[5,96,768]{2,1,0:T(8,128)S(1)}, f32[5,96,768]{2,1,0:T(8,128)}, u32[]{:S(2)}) copy-start(f32[5,96,768]{2,1,0:T(8,128)} %param.17) | copy-start | bytes 4423684

commit v2 on v1

--- a/solution.py
+++ b/solution.py
@@ -37,11 +37,29 @@
     return lax.ppermute(edge, "seq", pairs)
 
 
+def row_exchange(activated):
+    pairs = lambda step: [(j, j ^ step) for j in range(4)]
+    across = lax.ppermute(activated, "crow", pairs(1))
+    along = lax.ppermute(activated, "crow", pairs(2))
+    half = activated.shape[0] // 2
+    first = lax.ppermute(across[:half], "crow", pairs(2))
+    second = lax.ppermute(along[half:], "crow", pairs(1))
+    diagonal = jnp.concatenate([first, second], axis=0)
+    return jnp.stack([activated, across, along, diagonal])
+
+
 def convolution_block(inputs, bn_scale, bn_shift, conv_bias, kernel, dilation):
     activated = jax.nn.gelu(inputs * bn_scale[:, None] + bn_shift[:, None], approximate=False)
-    by_row = gathered(activated, "crow")
-    other_core = swap_ccol(by_row)
     core = lax.axis_index("ccol")
+    if lax.axis_size("crow") == 4 and activated.shape[0] % 2 == 0:
+        slots = row_exchange(activated)
+        other_slots = swap_ccol(slots)
+        row = lax.axis_index("crow")
+        by_row = jnp.stack([jnp.take(slots, jnp.bitwise_xor(row, r), axis=0) for r in range(4)])
+        other_core = jnp.stack([jnp.take(other_slots, jnp.bitwise_xor(row, r), axis=0) for r in range(4)])
+    else:
+        by_row = gathered(activated, "crow")
+        other_core = swap_ccol(by_row)
     tap_count, out_count, in_count = kernel.shape
     row_count, batch_count, block, rows = by_row.shape
     slot = lax.broadcasted_iota(jnp.int32, (1, 2, 1, 1, 1), 1)

time: 249 us -> 232 us (0.932)
  blocking collectives: 125 us -> 44.9 us
  waiting for transfers between devices: 52.6 us -> 97.4 us
  starting transfers between devices: 19.7 us -> 31.3 us
  other arithmetic: 13.7 us -> 20.9 us
    all_to_all x2 -> x0, blocking collectives: 80.2 us -> none  [gathered(): return lax.all_to_all(copies, axis_name, 0, 0, tiled=True)]
    ppermute x0 -> x8, waiting for transfers between devices: none -> 47.2 us  [the longest x2 32.4 us: row_exchange(): along = lax.ppermute(activated, 'crow', pairs(2))]
    ppermute x0 -> x8, starting transfers between devices: none -> 11.7 us  [the longest x2 4.62 us: row_exchange(): along = lax.ppermute(activated, 'crow', pairs(2))]
    select_n x0 -> x4, other arithmetic: none -> 4.93 us  [the longest x2 2.49 us: convolution_block(): jnp.take(other_slots, jnp.bitwise_xor(row, r), axis=0)]
    another operation x0 -> x5, other arithmetic: none -> 4.21 us  [row_exchange(): return jnp.stack([activated, across, along, diagonal])]
    select_n x2, other arithmetic: 4.68 us -> 1.9 us  [convolution_block(): ordered = jnp.where(slot == core, by_row[:, None], other_core[:, None])]
    unnamed x25 -> x29, local copies, waits for them, and re-layouts: 5.46 us -> 5.87 us
  transfers between devices with their start and end apart: 8 -> 16, of which waited for: 8 -> 15; matrix products, arithmetic and copies ran while one was open for 4% -> 6% of each run, Pallas kernels for 0% -> 0%
where the time goes in v2:
time: 232 us
  waiting for transfers between devices  97.4 us (42%)
  blocking collectives  44.9 us (19%)
  starting transfers between devices  31.3 us (13%)
  other arithmetic  20.9 us (9%)
  matrix products  20.1 us (9%)
  local copies, waits for them, and re-layouts  16 us (7%)
    ppermute x2, waiting for transfers between devices, row_exchange(): along = lax.ppermute(activated, 'crow', pairs(2))  32.4 us
    all_to_all x2, waiting for transfers between devices, gathered(): return lax.all_to_all(copies, axis_name, 0, 0, tiled=True)  24.7 us
    all_to_all x1, blocking collectives, attention_by_batch(): summed = jnp.sum(lax.all_to_all(shares, CHANNELS, 0, 0, tiled=True), axis=0)  23.5 us
    ppermute x4, waiting for transfers between devices, shifted_in(): return lax.ppermute(edge, 'seq', pairs)  16.6 us
    ppermute x2, waiting for transfers between devices, row_exchange(): second = lax.ppermute(along[half:], 'crow', pairs(1))  12.6 us
    ppermute x4, starting transfers between devices, shifted_in(): return lax.ppermute(edge, 'seq', pairs)  12.4 us
    all_to_all x1, blocking collectives, attention_by_batch(): lax.all_to_all(pooled.reshape(seq, per, pooled_rows, channels), 'seq', 0,...  11.7 us
    dot_general x2, matrix products, convolution_block(): jnp.einsum('btc,koc->kbto', ordered, kernel, precision=MATMUL_PRECISION)  10.9 us
  transfers between devices with their start and end apart: 16, of which 15 were waited for; matrix products, arithmetic and copies ran while one was open for 6% of the time, Pallas kernels for 0%

profile of v2, /device:TPU:0, one launch (start us, length us, event | category | flops | bytes accessed | tf_op | source)
XLA Modules:
  0.0 231.8 jit_solution(13977031636315743278)
XLA Ops:
  0.7 3.1 %fusion.36 = f32[8,96,256]{2,1,0:T(8,128)S(1)} fusion(f32[8,96,256]{2,1,0:T(8,128)} %param.15, f32[96]{0:T(128)} %param.17, f32[96]{0:T(128)} %param.16), kind=kLoop, calls=%fused_computation.53 | loop fusion | flops 12976128 | bytes 1573632 | tf_op jit(solution)/shard_map/mul | solution.py:52
  3.8 3.0 %collective-permute-start.1 = (f32[8,96,256]{2,1,0:T(8,128)S(1)}, f32[8,96,256]{2,1,0:T(8,128)S(1)}, u32[]{:S(2)}, u32[]{:S(2)}) collective-permute-start(f32[8,96,256]{2,1,0:T(8,128)S(1)} %fusion.36), channel_id=1, source_target_pairs={{0,4},{2,6},{4,0},{6,2},{1,5},{3,7},{5,1},{7,3},{8,12},{10,14},{12... | collective-permute-start | bytes 2359304 | tf_op jit(solution)/shard_map/ppermute | solution.py:43
  8.3 16.0 %collective-permute-done.1 = f32[8,96,256]{2,1,0:T(8,128)S(1)} collective-permute-done((f32[8,96,256]{2,1,0:T(8,128)S(1)}, f32[8,96,256]{2,1,0:T(8,128)S(1)}, u32[]{:S(2)}, u32[]{:S(2)}) %collective-permute-start.1) | collective-permute-done | bytes 786464 | tf_op jit(solution)/shard_map/ppermute | solution.py:43
  24.4 1.8 collective-permute-start.3
  26.2 1.6 collective-permute-start.2
  27.8 1.8 fusion.76
  29.6 5.2 %collective-permute-done.3 = f32[4,96,256]{2,1,0:T(8,128)S(1)} collective-permute-done((f32[4,96,256]{2,1,0:T(8,128)S(1)}, f32[4,96,256]{2,1,0:T(8,128)S(1)}, u32[]{:S(2)}, u32[]{:S(2)}) %collective-permute-start.3) | collective-permute-done | bytes 393248 | tf_op jit(solution)/shard_map/ppermute | solution.py:46
  36.0 2.0 pad_maximum_fusion
  38.2 2.1 dynamic-slice_select_fusion.15
  40.3 3.7 %collective-permute-done.4 = f32[4,8,96,256]{3,2,1,0:T(8,128)} collective-permute-done((f32[4,8,96,256]{3,2,1,0:T(8,128)}, f32[4,8,96,256]{3,2,1,0:T(8,128)}, u32[]{:S(2)}, u32[]{:S(2)}) %collective-permute-start.4) | collective-permute-done | bytes 3145760 | tf_op jit(solution)/shard_map/ppermute | solution.py:28
  44.0 2.1 dynamic-slice_select_fusion.11
  47.5 5.5 %fusion.10 = f32[5,8,256,96]{2,3,0,1:T(8,128)S(1)} fusion(f32[8,256,768]{1,2,0:T(8,128)S(1)} %bitcast_select_fusion.1, f32[5,96,768]{2,1,0:T(8,128)S(1)} %copy-done), kind=kOutput, calls=%fused_computation.26 | convolution fusion | flops 4529848320 | bytes 11698176 | tf_op jit(solution)/shard_map/btc,koc->kbto/dot_general | solution.py:68
  55.9 4.6 %collective-permute-start.5 = (f32[8,4,96]{1,2,0:T(8,128)S(1)}, f32[8,4,96]{1,2,0:T(8,128)S(1)}, u32[]{:S(2)}, u32[]{:S(2)}) collective-permute-start(f32[8,4,96]{1,2,0:T(8,128)S(1)} %get-tuple-element.34), channel_id=1, source_target_pairs={{0,8},{8,16},{16,24},{1,9},{9,17},{17,25},{2,10},{10,18},{18,26},{... | collective-permute-start | bytes 36872 | tf_op jit(solution)/shard_map/ppermute | solution.py:37
  60.6 7.1 %collective-permute-done.6 = f32[8,4,96]{1,2,0:T(8,128)S(1)} collective-permute-done((f32[8,4,96]{1,2,0:T(8,128)S(1)}, f32[8,4,96]{1,2,0:T(8,128)S(1)}, u32[]{:S(2)}, u32[]{:S(2)}) %collective-permute-start.6) | collective-permute-done | bytes 12320 | tf_op jit(solution)/shard_map/ppermute | solution.py:37
  68.9 2.0 fusion.38
  72.9 16.4 %collective-permute-done.8 = f32[8,96,256]{2,1,0:T(8,128)S(1)} collective-permute-done((f32[8,96,256]{2,1,0:T(8,128)S(1)}, f32[8,96,256]{2,1,0:T(8,128)S(1)}, u32[]{:S(2)}, u32[]{:S(2)}) %collective-permute-start.8) | collective-permute-done | bytes 786464 | tf_op jit(solution)/shard_map/ppermute | solution.py:43
  91.6 7.4 %collective-permute-done.10 = f32[4,96,256]{2,1,0:T(8,128)S(1)} collective-permute-done((f32[4,96,256]{2,1,0:T(8,128)S(1)}, f32[4,96,256]{2,1,0:T(8,128)S(1)}, u32[]{:S(2)}, u32[]{:S(2)}) %collective-permute-start.10) | collective-permute-done | bytes 393248 | tf_op jit(solution)/shard_map/ppermute | solution.py:46
  100.2 5.3 %collective-permute-done.11 = f32[4,8,96,256]{3,2,1,0:T(8,128)S(1)} collective-permute-done((f32[4,8,96,256]{3,2,1,0:T(8,128)S(1)}, f32[4,8,96,256]{3,2,1,0:T(8,128)S(1)}, u32[]{:S(2)}, u32[]{:S(2)}) %collective-permute-start.11) | collective-permute-done | bytes 3145760 | tf_op jit(solution)/shard_map/ppermute | solution.py:28
  107.6 5.4 %fusion.7 = f32[5,8,256,96]{2,3,1,0:T(8,128)S(1)} fusion(f32[8,256,768]{1,2,0:T(8,128)S(1)} %bitcast_select_fusion, f32[5,96,768]{2,1,0:T(8,128)S(1)} %copy-done.5), kind=kOutput, calls=%fused_computation.25 | convolution fusion | flops 4529848320 | bytes 11698176 | tf_op jit(solution)/shard_map/btc,koc->kbto/dot_general | solution.py:68
  115.8 5.3 %collective-permute-start.12 = (f32[8,8,96]{1,2,0:T(8,128)S(1)}, f32[8,8,96]{1,2,0:T(8,128)S(1)}, u32[]{:S(2)}, u32[]{:S(2)}) collective-permute-start(f32[8,8,96]{1,2,0:T(8,128)S(1)} %get-tuple-element.32), channel_id=1, source_target_pairs={{0,8},{8,16},{16,24},{1,9},{9,17},{17,25},{2,10},{10,18},{18,26},{... | collective-permute-start | bytes 73736 | tf_op jit(solution)/shard_map/ppermute | solution.py:37
  121.1 7.1 %collective-permute-done.13 = f32[8,8,96]{1,2,0:T(8,128)S(1)} collective-permute-done((f32[8,8,96]{1,2,0:T(8,128)S(1)}, f32[8,8,96]{1,2,0:T(8,128)S(1)}, u32[]{:S(2)}, u32[]{:S(2)}) %collective-permute-start.13) | collective-permute-done | bytes 24608 | tf_op jit(solution)/shard_map/ppermute | solution.py:37
  130.5 11.7 %all_to_all.25 = f32[4,2,32,96]{3,2,1,0:T(8,128)S(1)} all-to-all(f32[4,2,32,96]{3,2,1,0:T(8,128)S(1)} %bitcast.148), channel_id=1, replica_groups=mesh['seq'=4,'crow'=4,'ccol'=2] {'seq'}, dimensions={0} | all-to-all | bytes 196608 | tf_op jit(solution)/shard_map/all_to_all | solution.py:151
  143.3 3.5 %all-to-all-start.1 = ((f32[8,2,96,128]{3,2,1,0:T(8,128)}), f32[8,2,96,128]{3,2,1,0:T(8,128)S(1)}, u32[]{:S(2)}, u32[]{:S(2)}) async-start(f32[8,2,96,128]{3,2,1,0:T(8,128)} %broadcast_in_dim.123), calls=%async_computation.1 | async-start | bytes 1572864 | tf_op jit(solution)/shard_map/all_to_all | solution.py:20
  148.3 11.1 %all-to-all-done.1 = f32[8,2,96,128]{3,2,1,0:T(8,128)S(1)} async-done(((f32[8,2,96,128]{3,2,1,0:T(8,128)}), f32[8,2,96,128]{3,2,1,0:T(8,128)S(1)}, u32[]{:S(2)}, u32[]{:S(2)}) %all-to-all-start.1) | async-done | bytes 786464 | tf_op jit(solution)/shard_map/all_to_all | solution.py:20
  161.9 3.6 %all-to-all-start.2 = ((f32[8,2,192,128]{3,2,1,0:T(8,128)}), f32[8,2,192,128]{3,2,1,0:T(8,128)S(1)}, u32[]{:S(2)}, u32[]{:S(2)}) async-start(f32[8,2,192,128]{3,2,1,0:T(8,128)} %broadcast_in_dim.125), calls=%async_computation.2 | async-start | bytes 3145728 | tf_op jit(solution)/shard_map/all_to_all | solution.py:20
  165.5 5.4 %copy.65 = f32[1536,576]{1,0:T(8,128)} copy(f32[1536,576]{0,1:T(8,128)} %param.26) | data formatting | bytes 7077888 | tf_op args[11]
  171.0 1.6 copy.89
  172.9 13.6 %all-to-all-done.2 = f32[8,2,192,128]{3,2,1,0:T(8,128)S(1)} async-done(((f32[8,2,192,128]{3,2,1,0:T(8,128)}), f32[8,2,192,128]{3,2,1,0:T(8,128)S(1)}, u32[]{:S(2)}, u32[]{:S(2)}) %all-to-all-start.2) | async-done | bytes 1572896 | tf_op jit(solution)/shard_map/all_to_all | solution.py:20
  186.8 1.8 reshape.144
  188.6 6.9 %fusion.18 = f32[2,128,576]{1,2,0:T(8,128)S(1)} fusion(f32[8,192,576,1]{2,1,3,0:T(8,128)} %bitcast.139, f32[8,2,128,192]{3,2,1,0:T(8,128)} %reshape.144, f32[8,192]{1,0:T(8,128)S(1)} %mul.194, f32[2,128]{1,0:T(2,128)S(1)} %add_sqrt_fusion), kind=kOutput, calls=%fused_computation.32 | convolution fusion | flops 1359495168 | bytes 5708800 | tf_op jit(solution)/shard_map/nbtj,njo->bto/dot_general | solution.py:134
  197.4 23.5 %all_to_all.26 = f32[8,2,128,192]{2,3,1,0:T(8,128)S(1)} all-to-all(f32[8,2,128,192]{2,3,1,0:T(8,128)S(1)} %copy.69), channel_id=1, replica_groups=mesh['seq'=4,'crow'=4,'ccol'=2] {'crow','ccol'}, dimensions={0} | all-to-all | bytes 3145728 | tf_op jit(solution)/shard_map/all_to_all | solution.py:172
  221.4 9.7 %all_to_all.27 = f32[4,2,48,128]{3,2,1,0:T(8,128)S(1)} all-to-all(f32[4,2,48,128]{3,2,1,0:T(8,128)S(1)} %copy.72), channel_id=1, replica_groups=mesh['seq'=4,'crow'=4,'ccol'=2] {'seq'}, dimensions={0} | all-to-all | bytes 393216 | tf_op jit(solution)/shard_map/all_to_all | solution.py:174
  (97 shorter events, 29.7 us)
Async XLA Ops:
  0.6 46.8 %copy-start = (f32[5,96,768]{2,1,0:T(8,128)S(1)}, f32[5,96,768]{2,1,0:T(8,128)}, u32[]{:S(2)}) copy-start(f32[5,96,768]{2,1,0:T(8,128)} %param.19) | copy-start | bytes 4423684
  0.6 27.1 %copy-start.2 = (f32[8,96,256]{2,1,0:T(8,128)S(1)}, f32[8,96,256]{2,1,0:T(8,128)}, u32[]{:S(2)}) copy-start(f32[8,96,256]{2,1,0:T(8,128)} %param.15) | copy-start | bytes 2359300
  0.7 27.1 %copy-start.8 = (f32[96]{0:T(128)S(1)}, f32[96]{0:T(128)}, u32[]{:S(2)}) copy-start(f32[96]{0:T(128)} %param.17) | copy-start | bytes 1156
  0.7 27.1 %copy-start.9 = (f32[96]{0:T(128)S(1)}, f32[96]{0:T(128)}, u32[]{:S(2)}) copy-start(f32[96]{0:T(128)} %param.16) | copy-start | bytes 1156
  3.8 20.6 %collective-permute-start.1 = (f32[8,96,256]{2,1,0:T(8,128)S(1)}, f32[8,96,256]{2,1,0:T(8,128)S(1)}, u32[]{:S(2)}, u32[]{:S(2)}) collective-permute-start(f32[8,96,256]{2,1,0:T(8,128)S(1)} %fusion.36), channel_id=1, source_target_pairs={{0,4},{2,6},{4,0},{6,2},{1,5},{3,7},{5,1},{7,3},{8,12},{10,14},{12... | collective-permute-start | bytes 2359304 | tf_op jit(solution)/shard_map/ppermute | solution.py:43
  6.8 19.4 %collective-permute-start = (f32[8,96,256]{2,1,0:T(8,128)S(1)}, f32[8,96,256]{2,1,0:T(8,128)S(1)}, u32[]{:S(2)}, u32[]{:S(2)}) collective-permute-start(f32[8,96,256]{2,1,0:T(8,128)S(1)} %fusion.36), channel_id=1, source_target_pairs={{0,2},{2,0},{4,6},{6,4},{1,3},{3,1},{5,7},{7,5},{8,10},{10,8},{12,... | collective-permute-start | bytes 2359304 | tf_op jit(solution)/shard_map/ppermute | solution.py:42
  24.4 10.4 %collective-permute-start.3 = (f32[4,96,256]{2,1,0:T(8,128)S(1)}, f32[4,96,256]{2,1,0:T(8,128)S(1)}, u32[]{:S(2)}, u32[]{:S(2)}) collective-permute-start(f32[4,96,256]{2,1,0:T(8,128)S(1)} %slice.118), channel_id=1, source_target_pairs={{0,2},{2,0},{4,6},{6,4},{1,3},{3,1},{5,7},{7,5},{8,10},{10,8},{12,... | collective-permute-start | bytes 1179656 | tf_op jit(solution)/shard_map/ppermute | solution.py:46
  26.2 9.8 %collective-permute-start.2 = (f32[4,96,256]{2,1,0:T(8,128)S(1)}, f32[4,96,256]{2,1,0:T(8,128)S(1)}, u32[]{:S(2)}, u32[]{:S(2)}) collective-permute-start(f32[4,96,256]{2,1,0:T(8,128)S(1)} %slice.117), channel_id=1, source_target_pairs={{0,4},{2,6},{4,0},{6,2},{1,5},{3,7},{5,1},{7,3},{8,12},{10,14},{12... | collective-permute-start | bytes 1179656 | tf_op jit(solution)/shard_map/ppermute | solution.py:45
  38.0 6.0 %collective-permute-start.4 = (f32[4,8,96,256]{3,2,1,0:T(8,128)}, f32[4,8,96,256]{3,2,1,0:T(8,128)}, u32[]{:S(2)}, u32[]{:S(2)}) collective-permute-start(f32[4,8,96,256]{3,2,1,0:T(8,128)} %pad_maximum_fusion), channel_id=1, source_target_pairs={{0,1},{1,0},{2,3},{3,2},{4,5},{5,4},{6,7},{7,6},{8,9},{9,8},{10,11... | collective-permute-start | bytes 9437192 | tf_op jit(solution)/shard_map/ppermute | solution.py:28
  53.0 15.9 %copy-start.11 = (f32[96]{0:T(128)S(1)}, f32[96]{0:T(128)}, u32[]{:S(2)}) copy-start(f32[96]{0:T(128)} %param.21) | copy-start | bytes 1156
  53.0 15.9 %copy-start.12 = (f32[96]{0:T(128)S(1)}, f32[96]{0:T(128)}, u32[]{:S(2)}) copy-start(f32[96]{0:T(128)} %param.20) | copy-start | bytes 1156
  53.0 15.9 %copy-start.13 = (f32[96]{0:T(128)S(1)}, f32[96]{0:T(128)}, u32[]{:S(2)}) copy-start(f32[96]{0:T(128)} %param.18) | copy-start | bytes 1156
  54.6 13.0 %collective-permute-start.6 = (f32[8,4,96]{1,2,0:T(8,128)S(1)}, f32[8,4,96]{1,2,0:T(8,128)S(1)}, u32[]{:S(2)}, u32[]{:S(2)}) collective-permute-start(f32[8,4,96]{1,2,0:T(8,128)S(1)} %get-tuple-element.35), channel_id=1, source_target_pairs={{8,0},{16,8},{24,16},{9,1},{17,9},{25,17},{10,2},{18,10},{26,18},{... | collective-permute-start | bytes 36872 | tf_op jit(solution)/shard_map/ppermute | solution.py:37
  55.9 12.9 %collective-permute-start.5 = (f32[8,4,96]{1,2,0:T(8,128)S(1)}, f32[8,4,96]{1,2,0:T(8,128)S(1)}, u32[]{:S(2)}, u32[]{:S(2)}) collective-permute-start(f32[8,4,96]{1,2,0:T(8,128)S(1)} %get-tuple-element.34), channel_id=1, source_target_pairs={{0,8},{8,16},{16,24},{1,9},{9,17},{17,25},{2,10},{10,18},{18,26},{... | collective-permute-start | bytes 36872 | tf_op jit(solution)/shard_map/ppermute | solution.py:37
  70.8 18.5 %collective-permute-start.8 = (f32[8,96,256]{2,1,0:T(8,128)S(1)}, f32[8,96,256]{2,1,0:T(8,128)S(1)}, u32[]{:S(2)}, u32[]{:S(2)}) collective-permute-start(f32[8,96,256]{2,1,0:T(8,128)S(1)} %get-tuple-element.14), channel_id=1, source_target_pairs={{0,4},{2,6},{4,0},{6,2},{1,5},{3,7},{5,1},{7,3},{8,12},{10,14},{12... | collective-permute-start | bytes 2359304 | tf_op jit(solution)/shard_map/ppermute | solution.py:43
  72.4 18.6 %collective-permute-start.7 = (f32[8,96,256]{2,1,0:T(8,128)S(1)}, f32[8,96,256]{2,1,0:T(8,128)S(1)}, u32[]{:S(2)}, u32[]{:S(2)}) collective-permute-start(f32[8,96,256]{2,1,0:T(8,128)S(1)} %get-tuple-element.14), channel_id=1, source_target_pairs={{0,2},{2,0},{4,6},{6,4},{1,3},{3,1},{5,7},{7,5},{8,10},{10,8},{12,... | collective-permute-start | bytes 2359304 | tf_op jit(solution)/shard_map/ppermute | solution.py:42
  89.4 9.6 %collective-permute-start.10 = (f32[4,96,256]{2,1,0:T(8,128)S(1)}, f32[4,96,256]{2,1,0:T(8,128)S(1)}, u32[]{:S(2)}, u32[]{:S(2)}) collective-permute-start(f32[4,96,256]{2,1,0:T(8,128)S(1)} %slice.123), channel_id=1, source_target_pairs={{0,2},{2,0},{4,6},{6,4},{1,3},{3,1},{5,7},{7,5},{8,10},{10,8},{12,... | collective-permute-start | bytes 1179656 | tf_op jit(solution)/shard_map/ppermute | solution.py:46
  91.0 8.5 %collective-permute-start.9 = (f32[4,96,256]{2,1,0:T(8,128)S(1)}, f32[4,96,256]{2,1,0:T(8,128)S(1)}, u32[]{:S(2)}, u32[]{:S(2)}) collective-permute-start(f32[4,96,256]{2,1,0:T(8,128)S(1)} %slice.122), channel_id=1, source_target_pairs={{0,4},{2,6},{4,0},{6,2},{1,5},{3,7},{5,1},{7,3},{8,12},{10,14},{12... | collective-permute-start | bytes 1179656 | tf_op jit(solution)/shard_map/ppermute | solution.py:45
  99.8 5.7 %collective-permute-start.11 = (f32[4,8,96,256]{3,2,1,0:T(8,128)S(1)}, f32[4,8,96,256]{3,2,1,0:T(8,128)S(1)}, u32[]{:S(2)}, u32[]{:S(2)}) collective-permute-start(f32[4,8,96,256]{3,2,1,0:T(8,128)S(1)} %pad_maximum_fusion.1), channel_id=1, source_target_pairs={{0,1},{1,0},{2,3},{3,2},{4,5},{5,4},{6,7},{7,6},{8,9},{9,8},{10,11... | collective-permute-start | bytes 9437192 | tf_op jit(solution)/shard_map/ppermute | solution.py:28
  106.2 1.4 copy-start.5
  113.0 16.4 %copy-start.10 = (f32[96]{0:T(128)S(1)}, f32[96]{0:T(128)}, u32[]{:S(2)}) copy-start(f32[96]{0:T(128)} %param.22) | copy-start | bytes 1156
  114.5 13.8 %collective-permute-start.13 = (f32[8,8,96]{1,2,0:T(8,128)S(1)}, f32[8,8,96]{1,2,0:T(8,128)S(1)}, u32[]{:S(2)}, u32[]{:S(2)}) collective-permute-start(f32[8,8,96]{1,2,0:T(8,128)S(1)} %get-tuple-element.33), channel_id=1, source_target_pairs={{8,0},{16,8},{24,16},{9,1},{17,9},{25,17},{10,2},{18,10},{26,18},{... | collective-permute-start | bytes 73736 | tf_op jit(solution)/shard_map/ppermute | solution.py:37
  115.8 13.7 %collective-permute-start.12 = (f32[8,8,96]{1,2,0:T(8,128)S(1)}, f32[8,8,96]{1,2,0:T(8,128)S(1)}, u32[]{:S(2)}, u32[]{:S(2)}) collective-permute-start(f32[8,8,96]{1,2,0:T(8,128)S(1)} %get-tuple-element.32), channel_id=1, source_target_pairs={{0,8},{8,16},{16,24},{1,9},{9,17},{17,25},{2,10},{10,18},{18,26},{... | collective-permute-start | bytes 73736 | tf_op jit(solution)/shard_map/ppermute | solution.py:37
  129.9 13.4 %copy-start.4 = (f32[8,96,256]{2,1,0:T(8,128)}, f32[8,96,256]{2,1,0:T(8,128)S(1)}, u32[]{:S(2)}) copy-start(f32[8,96,256]{2,1,0:T(8,128)S(1)} %fusion.40) | copy-start | bytes 2359300
  143.3 16.1 %all-to-all-start.1 = ((f32[8,2,96,128]{3,2,1,0:T(8,128)}), f32[8,2,96,128]{3,2,1,0:T(8,128)S(1)}, u32[]{:S(2)}, u32[]{:S(2)}) async-start(f32[8,2,96,128]{3,2,1,0:T(8,128)} %broadcast_in_dim.123), calls=%async_computation.1 | async-start | bytes 1572864 | tf_op jit(solution)/shard_map/all_to_all | solution.py:20
  161.9 24.5 %all-to-all-start.2 = ((f32[8,2,192,128]{3,2,1,0:T(8,128)}), f32[8,2,192,128]{3,2,1,0:T(8,128)S(1)}, u32[]{:S(2)}, u32[]{:S(2)}) async-start(f32[8,2,192,128]{3,2,1,0:T(8,128)} %broadcast_in_dim.125), calls=%async_computation.2 | async-start | bytes 3145728 | tf_op jit(solution)/shard_map/all_to_all | solution.py:20
  165.5 5.4 %copy-start.7 = (f32[1536]{0:T(1024)S(1)}, f32[1536]{0:T(1024)}, u32[]{:S(2)}) copy-start(f32[1536]{0:T(1024)} %param.25) | copy-start | bytes 18436
  165.5 5.5 %copy-start.6 = (f32[192,1536]{1,0:T(8,128)S(1)}, f32[192,1536]{1,0:T(8,128)}, u32[]{:S(2)}) copy-start(f32[192,1536]{1,0:T(8,128)} %param.27) | copy-start | bytes 3538948
  188.6 7.8 %copy-start.3 = (f32[192,1536]{0,1:T(8,128)S(1)}, f32[192,1536]{0,1:T(8,128)}, u32[]{:S(2)}) copy-start(f32[192,1536]{0,1:T(8,128)} %copy.89) | copy-start | bytes 3538948
  197.2 34.6 %copy-start.1 = (f32[5,96,768]{2,1,0:T(8,128)S(1)}, f32[5,96,768]{2,1,0:T(8,128)}, u32[]{:S(2)}) copy-start(f32[5,96,768]{2,1,0:T(8,128)} %param.19) | copy-start | bytes 4423684

commit v3 on v2

--- a/solution.py
+++ b/solution.py
@@ -45,15 +45,15 @@
     first = lax.ppermute(across[:half], "crow", pairs(2))
     second = lax.ppermute(along[half:], "crow", pairs(1))
     diagonal = jnp.concatenate([first, second], axis=0)
-    return jnp.stack([activated, across, along, diagonal])
+    slots = [activated, across, along, diagonal]
+    return jnp.stack(slots), jnp.stack([swap_ccol(one) for one in slots])
 
 
 def convolution_block(inputs, bn_scale, bn_shift, conv_bias, kernel, dilation):
     activated = jax.nn.gelu(inputs * bn_scale[:, None] + bn_shift[:, None], approximate=False)
     core = lax.axis_index("ccol")
     if lax.axis_size("crow") == 4 and activated.shape[0] % 2 == 0:
-        slots = row_exchange(activated)
-        other_slots = swap_ccol(slots)
+        slots, other_slots = row_exchange(activated)
         row = lax.axis_index("crow")
         by_row = jnp.stack([jnp.take(slots, jnp.bitwise_xor(row, r), axis=0) for r in range(4)])
         other_core = jnp.stack([jnp.take(other_slots, jnp.bitwise_xor(row, r), axis=0) for r in range(4)])

time: 232 us -> 229 us (0.987)
  waiting for transfers between devices: 97.4 us -> 92.7 us
  local copies, waits for them, and re-layouts: 16 us -> 19.6 us
  other arithmetic: 20.9 us -> 18.1 us
    ppermute x2, waiting for transfers between devices: 0.46 us -> 33 us  [row_exchange(): across = lax.ppermute(activated, 'crow', pairs(1))]
    ppermute x2, waiting for transfers between devices: 32.4 us -> 0.57 us  [row_exchange(): along = lax.ppermute(activated, 'crow', pairs(2))]
    ppermute x2, waiting for transfers between devices: 1.68 us -> 11.7 us  [row_exchange(): first = lax.ppermute(across[:half], 'crow', pairs(2))]
    ppermute x2, waiting for transfers between devices: 12.6 us -> 3.75 us  [row_exchange(): second = lax.ppermute(along[half:], 'crow', pairs(1))]
    ppermute x2 -> x8, waiting for transfers between devices: 9.02 us -> 1.99 us  [swap_ccol(): return lax.ppermute(x, 'ccol', [(0, 1), (1, 0)])]
    ppermute x2, starting transfers between devices: 4.62 us -> 2.02 us  [row_exchange(): along = lax.ppermute(activated, 'crow', pairs(2))]
    ppermute x2, starting transfers between devices: 2.03 us -> 4.5 us  [row_exchange(): across = lax.ppermute(activated, 'crow', pairs(1))]
    unnamed x29 -> x35, local copies, waits for them, and re-layouts: 5.87 us -> 6.84 us
  transfers between devices with their start and end apart: 16 -> 22, of which waited for: 15 -> 14; matrix products, arithmetic and copies ran while one was open for 6% -> 6% of each run, Pallas kernels for 0% -> 0%
where the time goes in v3:
time: 229 us
  waiting for transfers between devices  92.7 us (40%)
  blocking collectives  44.9 us (20%)
  starting transfers between devices  32.2 us (14%)
  matrix products  20.1 us (9%)
  local copies, waits for them, and re-layouts  19.6 us (9%)
  other arithmetic  18.1 us (8%)
    ppermute x2, waiting for transfers between devices, row_exchange(): across = lax.ppermute(activated, 'crow', pairs(1))  33 us
    all_to_all x2, waiting for transfers between devices, gathered(): return lax.all_to_all(copies, axis_name, 0, 0, tiled=True)  24.7 us
    all_to_all x1, blocking collectives, attention_by_batch(): summed = jnp.sum(lax.all_to_all(shares, CHANNELS, 0, 0, tiled=True), axis=0)  23.5 us
    ppermute x4, waiting for transfers between devices, shifted_in(): return lax.ppermute(edge, 'seq', pairs)  16.9 us
    ppermute x4, starting transfers between devices, shifted_in(): return lax.ppermute(edge, 'seq', pairs)  12.4 us
    ppermute x2, waiting for transfers between devices, row_exchange(): first = lax.ppermute(across[:half], 'crow', pairs(2))  11.7 us
    all_to_all x1, blocking collectives, attention_by_batch(): lax.all_to_all(pooled.reshape(seq, per, pooled_rows, channels), 'seq', 0,...  11.7 us
    dot_general x2, matrix products, convolution_block(): jnp.einsum('btc,koc->kbto', ordered, kernel, precision=MATMUL_PRECISION)  10.9 us
  transfers between devices with their start and end apart: 22, of which 14 were waited for; matrix products, arithmetic and copies ran while one was open for 6% of the time, Pallas kernels for 0%

profile of v3, /device:TPU:0, one launch (start us, length us, event | category | flops | bytes accessed | tf_op | source)
XLA Modules:
  0.0 228.8 jit_solution(11215904428517466731)
XLA Ops:
  0.7 4.0 %fusion.36 = f32[8,96,256]{2,1,0:T(8,128)} fusion(f32[8,96,256]{2,1,0:T(8,128)} %param.15, f32[96]{0:T(128)} %param.17, f32[96]{0:T(128)} %param.16), kind=kLoop, calls=%fused_computation.55 | loop fusion | flops 12976128 | bytes 1573632 | tf_op jit(solution)/shard_map/mul | solution.py:53
  4.6 2.9 %collective-permute-start = (f32[8,96,256]{2,1,0:T(8,128)}, f32[8,96,256]{2,1,0:T(8,128)S(1)}, u32[]{:S(2)}, u32[]{:S(2)}) collective-permute-start(f32[8,96,256]{2,1,0:T(8,128)} %fusion.36), channel_id=1, source_target_pairs={{0,2},{2,0},{4,6},{6,4},{1,3},{3,1},{5,7},{7,5},{8,10},{10,8},{12,... | collective-permute-start | bytes 2359304 | tf_op jit(solution)/shard_map/ppermute | solution.py:42
  7.6 1.5 collective-permute-start.1
  9.1 16.2 %collective-permute-done = f32[8,96,256]{2,1,0:T(8,128)S(1)} collective-permute-done((f32[8,96,256]{2,1,0:T(8,128)}, f32[8,96,256]{2,1,0:T(8,128)S(1)}, u32[]{:S(2)}, u32[]{:S(2)}) %collective-permute-start) | collective-permute-done | bytes 786464 | tf_op jit(solution)/shard_map/ppermute | solution.py:42
  26.1 1.8 collective-permute-start.2
  29.6 1.5 collective-permute-start.3
  31.9 4.8 %collective-permute-done.2 = f32[4,96,256]{2,1,0:T(8,128)S(1)} collective-permute-done((f32[4,96,256]{2,1,0:T(8,128)}, f32[4,96,256]{2,1,0:T(8,128)S(1)}, u32[]{:S(2)}, u32[]{:S(2)}) %collective-permute-start.2) | collective-permute-done | bytes 393248 | tf_op jit(solution)/shard_map/ppermute | solution.py:45
  36.7 2.9 %collective-permute-done.3 = f32[4,96,256]{2,1,0:T(8,128)} collective-permute-done((f32[4,96,256]{2,1,0:T(8,128)}, f32[4,96,256]{2,1,0:T(8,128)}, u32[]{:S(2)}, u32[]{:S(2)}) %collective-permute-start.3) | collective-permute-done | bytes 393248 | tf_op jit(solution)/shard_map/ppermute | solution.py:46
  40.7 1.8 fusion.76
  46.1 5.5 %fusion.10 = f32[5,8,256,96]{2,3,0,1:T(8,128)S(1)} fusion(f32[8,256,768]{1,2,0:T(8,128)S(1)} %bitcast_select_fusion.1, f32[5,96,768]{2,1,0:T(8,128)S(1)} %copy-done), kind=kOutput, calls=%fused_computation.28 | convolution fusion | flops 4529848320 | bytes 11698176 | tf_op jit(solution)/shard_map/btc,koc->kbto/dot_general | solution.py:68
  51.7 1.5 fusion.25
  54.6 4.6 %collective-permute-start.8 = (f32[8,4,96]{1,2,0:T(8,128)S(1)}, f32[8,4,96]{1,2,0:T(8,128)S(1)}, u32[]{:S(2)}, u32[]{:S(2)}) collective-permute-start(f32[8,4,96]{1,2,0:T(8,128)S(1)} %get-tuple-element.34), channel_id=1, source_target_pairs={{0,8},{8,16},{16,24},{1,9},{9,17},{17,25},{2,10},{10,18},{18,26},{... | collective-permute-start | bytes 36872 | tf_op jit(solution)/shard_map/ppermute | solution.py:37
  59.3 7.4 %collective-permute-done.9 = f32[8,4,96]{1,2,0:T(8,128)S(1)} collective-permute-done((f32[8,4,96]{1,2,0:T(8,128)S(1)}, f32[8,4,96]{1,2,0:T(8,128)S(1)}, u32[]{:S(2)}, u32[]{:S(2)}) %collective-permute-start.9) | collective-permute-done | bytes 12320 | tf_op jit(solution)/shard_map/ppermute | solution.py:37
  67.9 2.0 fusion.38
  69.9 1.6 collective-permute-start.10
  71.9 16.8 %collective-permute-done.10 = f32[8,96,256]{2,1,0:T(8,128)S(1)} collective-permute-done((f32[8,96,256]{2,1,0:T(8,128)S(1)}, f32[8,96,256]{2,1,0:T(8,128)S(1)}, u32[]{:S(2)}, u32[]{:S(2)}) %collective-permute-start.10) | collective-permute-done | bytes 786464 | tf_op jit(solution)/shard_map/ppermute | solution.py:42
  91.4 6.9 %collective-permute-done.12 = f32[4,96,256]{2,1,0:T(8,128)S(1)} collective-permute-done((f32[4,96,256]{2,1,0:T(8,128)S(1)}, f32[4,96,256]{2,1,0:T(8,128)S(1)}, u32[]{:S(2)}, u32[]{:S(2)}) %collective-permute-start.12) | collective-permute-done | bytes 393248 | tf_op jit(solution)/shard_map/ppermute | solution.py:45
  99.7 2.0 collective-permute-done.17
  104.5 5.4 %fusion.7 = f32[5,8,256,96]{2,3,1,0:T(8,128)S(1)} fusion(f32[8,256,768]{1,2,0:T(8,128)S(1)} %bitcast_select_fusion, f32[5,96,768]{2,1,0:T(8,128)S(1)} %copy-done.7), kind=kOutput, calls=%fused_computation.27 | convolution fusion | flops 4529848320 | bytes 11698176 | tf_op jit(solution)/shard_map/btc,koc->kbto/dot_general | solution.py:68
  112.7 5.3 %collective-permute-start.18 = (f32[8,8,96]{1,2,0:T(8,128)S(1)}, f32[8,8,96]{1,2,0:T(8,128)S(1)}, u32[]{:S(2)}, u32[]{:S(2)}) collective-permute-start(f32[8,8,96]{1,2,0:T(8,128)S(1)} %get-tuple-element.32), channel_id=1, source_target_pairs={{0,8},{8,16},{16,24},{1,9},{9,17},{17,25},{2,10},{10,18},{18,26},{... | collective-permute-start | bytes 73736 | tf_op jit(solution)/shard_map/ppermute | solution.py:37
  118.0 7.1 %collective-permute-done.19 = f32[8,8,96]{1,2,0:T(8,128)S(1)} collective-permute-done((f32[8,8,96]{1,2,0:T(8,128)S(1)}, f32[8,8,96]{1,2,0:T(8,128)S(1)}, u32[]{:S(2)}, u32[]{:S(2)}) %collective-permute-start.19) | collective-permute-done | bytes 24608 | tf_op jit(solution)/shard_map/ppermute | solution.py:37
  127.4 11.7 %all_to_all.25 = f32[4,2,32,96]{3,2,1,0:T(8,128)S(1)} all-to-all(f32[4,2,32,96]{3,2,1,0:T(8,128)S(1)} %bitcast.163), channel_id=1, replica_groups=mesh['seq'=4,'crow'=4,'ccol'=2] {'seq'}, dimensions={0} | all-to-all | bytes 196608 | tf_op jit(solution)/shard_map/all_to_all | solution.py:151
  140.2 3.5 %all-to-all-start.1 = ((f32[8,2,96,128]{3,2,1,0:T(8,128)}), f32[8,2,96,128]{3,2,1,0:T(8,128)S(1)}, u32[]{:S(2)}, u32[]{:S(2)}) async-start(f32[8,2,96,128]{3,2,1,0:T(8,128)} %broadcast_in_dim.123), calls=%async_computation.1 | async-start | bytes 1572864 | tf_op jit(solution)/shard_map/all_to_all | solution.py:20
  145.2 11.1 %all-to-all-done.1 = f32[8,2,96,128]{3,2,1,0:T(8,128)S(1)} async-done(((f32[8,2,96,128]{3,2,1,0:T(8,128)}), f32[8,2,96,128]{3,2,1,0:T(8,128)S(1)}, u32[]{:S(2)}, u32[]{:S(2)}) %all-to-all-start.1) | async-done | bytes 786464 | tf_op jit(solution)/shard_map/all_to_all | solution.py:20
  158.8 3.6 %all-to-all-start.2 = ((f32[8,2,192,128]{3,2,1,0:T(8,128)}), f32[8,2,192,128]{3,2,1,0:T(8,128)S(1)}, u32[]{:S(2)}, u32[]{:S(2)}) async-start(f32[8,2,192,128]{3,2,1,0:T(8,128)} %broadcast_in_dim.125), calls=%async_computation.2 | async-start | bytes 3145728 | tf_op jit(solution)/shard_map/all_to_all | solution.py:20
  162.4 5.4 %copy.65 = f32[1536,576]{1,0:T(8,128)} copy(f32[1536,576]{0,1:T(8,128)} %param.26) | data formatting | bytes 7077888 | tf_op args[11]
  167.9 1.6 copy.89
  169.8 13.6 %all-to-all-done.2 = f32[8,2,192,128]{3,2,1,0:T(8,128)S(1)} async-done(((f32[8,2,192,128]{3,2,1,0:T(8,128)}), f32[8,2,192,128]{3,2,1,0:T(8,128)S(1)}, u32[]{:S(2)}, u32[]{:S(2)}) %all-to-all-start.2) | async-done | bytes 1572896 | tf_op jit(solution)/shard_map/all_to_all | solution.py:20
  183.7 1.8 reshape.144
  185.5 6.9 %fusion.18 = f32[2,128,576]{1,2,0:T(8,128)S(1)} fusion(f32[8,192,576,1]{2,1,3,0:T(8,128)} %bitcast.145, f32[8,2,128,192]{3,2,1,0:T(8,128)} %reshape.144, f32[8,192]{1,0:T(8,128)S(1)} %mul.194, f32[2,128]{1,0:T(2,128)S(1)} %add_sqrt_fusion), kind=kOutput, calls=%fused_computation.34 | convolution fusion | flops 1359495168 | bytes 5708800 | tf_op jit(solution)/shard_map/nbtj,njo->bto/dot_general | solution.py:134
  194.3 23.5 %all_to_all.26 = f32[8,2,128,192]{2,3,1,0:T(8,128)S(1)} all-to-all(f32[8,2,128,192]{2,3,1,0:T(8,128)S(1)} %copy.69), channel_id=1, replica_groups=mesh['seq'=4,'crow'=4,'ccol'=2] {'crow','ccol'}, dimensions={0} | all-to-all | bytes 3145728 | tf_op jit(solution)/shard_map/all_to_all | solution.py:172
  218.3 9.7 %all_to_all.27 = f32[4,2,48,128]{3,2,1,0:T(8,128)S(1)} all-to-all(f32[4,2,48,128]{3,2,1,0:T(8,128)S(1)} %copy.72), channel_id=1, replica_groups=mesh['seq'=4,'crow'=4,'ccol'=2] {'seq'}, dimensions={0} | all-to-all | bytes 393216 | tf_op jit(solution)/shard_map/all_to_all | solution.py:174
  (116 shorter events, 31.6 us)
Async XLA Ops:
  0.6 45.5 %copy-start = (f32[5,96,768]{2,1,0:T(8,128)S(1)}, f32[5,96,768]{2,1,0:T(8,128)}, u32[]{:S(2)}) copy-start(f32[5,96,768]{2,1,0:T(8,128)} %param.19) | copy-start | bytes 4423684
  0.6 40.1 %copy-start.2 = (f32[8,96,256]{2,1,0:T(8,128)S(1)}, f32[8,96,256]{2,1,0:T(8,128)}, u32[]{:S(2)}) copy-start(f32[8,96,256]{2,1,0:T(8,128)} %param.15) | copy-start | bytes 2359300
  0.7 40.1 %copy-start.10 = (f32[96]{0:T(128)S(1)}, f32[96]{0:T(128)}, u32[]{:S(2)}) copy-start(f32[96]{0:T(128)} %param.17) | copy-start | bytes 1156
  0.7 40.1 %copy-start.11 = (f32[96]{0:T(128)S(1)}, f32[96]{0:T(128)}, u32[]{:S(2)}) copy-start(f32[96]{0:T(128)} %param.16) | copy-start | bytes 1156
  4.6 20.7 %collective-permute-start = (f32[8,96,256]{2,1,0:T(8,128)}, f32[8,96,256]{2,1,0:T(8,128)S(1)}, u32[]{:S(2)}, u32[]{:S(2)}) collective-permute-start(f32[8,96,256]{2,1,0:T(8,128)} %fusion.36), channel_id=1, source_target_pairs={{0,2},{2,0},{4,6},{6,4},{1,3},{3,1},{5,7},{7,5},{8,10},{10,8},{12,... | collective-permute-start | bytes 2359304 | tf_op jit(solution)/shard_map/ppermute | solution.py:42
  7.6 20.3 %collective-permute-start.1 = (f32[8,96,256]{2,1,0:T(8,128)}, f32[8,96,256]{2,1,0:T(8,128)S(1)}, u32[]{:S(2)}, u32[]{:S(2)}) collective-permute-start(f32[8,96,256]{2,1,0:T(8,128)} %fusion.36), channel_id=1, source_target_pairs={{0,4},{2,6},{4,0},{6,2},{1,5},{3,7},{5,1},{7,3},{8,12},{10,14},{12... | collective-permute-start | bytes 2359304 | tf_op jit(solution)/shard_map/ppermute | solution.py:43
  26.1 10.5 %collective-permute-start.2 = (f32[4,96,256]{2,1,0:T(8,128)}, f32[4,96,256]{2,1,0:T(8,128)S(1)}, u32[]{:S(2)}, u32[]{:S(2)}) collective-permute-start(f32[4,96,256]{2,1,0:T(8,128)} %slice.117), channel_id=1, source_target_pairs={{0,4},{2,6},{4,0},{6,2},{1,5},{3,7},{5,1},{7,3},{8,12},{10,14},{12... | collective-permute-start | bytes 1179656 | tf_op jit(solution)/shard_map/ppermute | solution.py:45
  29.6 10.0 %collective-permute-start.3 = (f32[4,96,256]{2,1,0:T(8,128)}, f32[4,96,256]{2,1,0:T(8,128)}, u32[]{:S(2)}, u32[]{:S(2)}) collective-permute-start(f32[4,96,256]{2,1,0:T(8,128)} %slice.118), channel_id=1, source_target_pairs={{0,2},{2,0},{4,6},{6,4},{1,3},{3,1},{5,7},{7,5},{8,10},{10,8},{12,... | collective-permute-start | bytes 1179656 | tf_op jit(solution)/shard_map/ppermute | solution.py:46
  31.1 12.1 %collective-permute-start.4 = (f32[8,96,256]{2,1,0:T(8,128)}, f32[8,96,256]{2,1,0:T(8,128)}, u32[]{:S(2)}, u32[]{:S(2)}) collective-permute-start(f32[8,96,256]{2,1,0:T(8,128)} %fusion.36), channel_id=1, source_target_pairs={{0,1},{1,0},{2,3},{3,2},{4,5},{5,4},{6,7},{7,6},{8,9},{9,8},{10,11... | collective-permute-start | bytes 2359304 | tf_op jit(solution)/shard_map/ppermute | solution.py:28
  31.2 11.9 %collective-permute-start.6 = (f32[8,96,256]{2,1,0:T(8,128)}, f32[8,96,256]{2,1,0:T(8,128)S(1)}, u32[]{:S(2)}, u32[]{:S(2)}) collective-permute-start(f32[8,96,256]{2,1,0:T(8,128)} %copy-done.5), channel_id=1, source_target_pairs={{0,1},{1,0},{2,3},{3,2},{4,5},{5,4},{6,7},{7,6},{8,9},{9,8},{10,11... | collective-permute-start | bytes 2359304 | tf_op jit(solution)/shard_map/ppermute | solution.py:28
  31.8 11.4 %collective-permute-start.5 = (f32[8,96,256]{2,1,0:T(8,128)S(1)}, f32[8,96,256]{2,1,0:T(8,128)S(1)}, u32[]{:S(2)}, u32[]{:S(2)}) collective-permute-start(f32[8,96,256]{2,1,0:T(8,128)S(1)} %collective-permute-done), channel_id=1, source_target_pairs={{0,1},{1,0},{2,3},{3,2},{4,5},{5,4},{6,7},{7,6},{8,9},{9,8},{10,11... | collective-permute-start | bytes 2359304 | tf_op jit(solution)/shard_map/ppermute | solution.py:28
  40.6 2.5 %collective-permute-start.7 = (f32[8,96,256]{2,1,0:T(8,128)S(1)}, f32[8,96,256]{2,1,0:T(8,128)S(1)}, u32[]{:S(2)}, u32[]{:S(2)}) collective-permute-start(f32[8,96,256]{2,1,0:T(8,128)S(1)} %constant_dynamic-update-slice_fusion), channel_id=1, source_target_pairs={{0,1},{1,0},{2,3},{3,2},{4,5},{5,4},{6,7},{7,6},{8,9},{9,8},{10,11... | collective-permute-start | bytes 2359304 | tf_op jit(solution)/shard_map/ppermute | solution.py:28
  51.6 16.2 %copy-start.13 = (f32[96]{0:T(128)S(1)}, f32[96]{0:T(128)}, u32[]{:S(2)}) copy-start(f32[96]{0:T(128)} %param.21) | copy-start | bytes 1156
  51.7 16.2 %copy-start.14 = (f32[96]{0:T(128)S(1)}, f32[96]{0:T(128)}, u32[]{:S(2)}) copy-start(f32[96]{0:T(128)} %param.20) | copy-start | bytes 1156
  51.7 16.2 %copy-start.15 = (f32[96]{0:T(128)S(1)}, f32[96]{0:T(128)}, u32[]{:S(2)}) copy-start(f32[96]{0:T(128)} %param.18) | copy-start | bytes 1156
  53.3 13.4 %collective-permute-start.9 = (f32[8,4,96]{1,2,0:T(8,128)S(1)}, f32[8,4,96]{1,2,0:T(8,128)S(1)}, u32[]{:S(2)}, u32[]{:S(2)}) collective-permute-start(f32[8,4,96]{1,2,0:T(8,128)S(1)} %get-tuple-element.35), channel_id=1, source_target_pairs={{8,0},{16,8},{24,16},{9,1},{17,9},{25,17},{10,2},{18,10},{26,18},{... | collective-permute-start | bytes 36872 | tf_op jit(solution)/shard_map/ppermute | solution.py:37
  54.6 13.3 %collective-permute-start.8 = (f32[8,4,96]{1,2,0:T(8,128)S(1)}, f32[8,4,96]{1,2,0:T(8,128)S(1)}, u32[]{:S(2)}, u32[]{:S(2)}) collective-permute-start(f32[8,4,96]{1,2,0:T(8,128)S(1)} %get-tuple-element.34), channel_id=1, source_target_pairs={{0,8},{8,16},{16,24},{1,9},{9,17},{17,25},{2,10},{10,18},{18,26},{... | collective-permute-start | bytes 36872 | tf_op jit(solution)/shard_map/ppermute | solution.py:37
  69.9 18.9 %collective-permute-start.10 = (f32[8,96,256]{2,1,0:T(8,128)S(1)}, f32[8,96,256]{2,1,0:T(8,128)S(1)}, u32[]{:S(2)}, u32[]{:S(2)}) collective-permute-start(f32[8,96,256]{2,1,0:T(8,128)S(1)} %get-tuple-element.14), channel_id=1, source_target_pairs={{0,2},{2,0},{4,6},{6,4},{1,3},{3,1},{5,7},{7,5},{8,10},{10,8},{12,... | collective-permute-start | bytes 2359304 | tf_op jit(solution)/shard_map/ppermute | solution.py:42
  71.4 18.6 %collective-permute-start.11 = (f32[8,96,256]{2,1,0:T(8,128)S(1)}, f32[8,96,256]{2,1,0:T(8,128)S(1)}, u32[]{:S(2)}, u32[]{:S(2)}) collective-permute-start(f32[8,96,256]{2,1,0:T(8,128)S(1)} %get-tuple-element.14), channel_id=1, source_target_pairs={{0,4},{2,6},{4,0},{6,2},{1,5},{3,7},{5,1},{7,3},{8,12},{10,14},{12... | collective-permute-start | bytes 2359304 | tf_op jit(solution)/shard_map/ppermute | solution.py:43
  88.8 9.6 %collective-permute-start.12 = (f32[4,96,256]{2,1,0:T(8,128)S(1)}, f32[4,96,256]{2,1,0:T(8,128)S(1)}, u32[]{:S(2)}, u32[]{:S(2)}) collective-permute-start(f32[4,96,256]{2,1,0:T(8,128)S(1)} %slice.122), channel_id=1, source_target_pairs={{0,4},{2,6},{4,0},{6,2},{1,5},{3,7},{5,1},{7,3},{8,12},{10,14},{12... | collective-permute-start | bytes 1179656 | tf_op jit(solution)/shard_map/ppermute | solution.py:45
  90.0 9.2 %collective-permute-start.13 = (f32[4,96,256]{2,1,0:T(8,128)S(1)}, f32[4,96,256]{2,1,0:T(8,128)S(1)}, u32[]{:S(2)}, u32[]{:S(2)}) collective-permute-start(f32[4,96,256]{2,1,0:T(8,128)S(1)} %slice.123), channel_id=1, source_target_pairs={{0,2},{2,0},{4,6},{6,4},{1,3},{3,1},{5,7},{7,5},{8,10},{10,8},{12,... | collective-permute-start | bytes 1179656 | tf_op jit(solution)/shard_map/ppermute | solution.py:46
  90.9 8.7 %collective-permute-start.14 = (f32[8,96,256]{2,1,0:T(8,128)S(1)}, f32[8,96,256]{2,1,0:T(8,128)S(1)}, u32[]{:S(2)}, u32[]{:S(2)}) collective-permute-start(f32[8,96,256]{2,1,0:T(8,128)S(1)} %get-tuple-element.14), channel_id=1, source_target_pairs={{0,1},{1,0},{2,3},{3,2},{4,5},{5,4},{6,7},{7,6},{8,9},{9,8},{10,11... | collective-permute-start | bytes 2359304 | tf_op jit(solution)/shard_map/ppermute | solution.py:28
  90.9 8.7 %collective-permute-start.16 = (f32[8,96,256]{2,1,0:T(8,128)S(1)}, f32[8,96,256]{2,1,0:T(8,128)S(1)}, u32[]{:S(2)}, u32[]{:S(2)}) collective-permute-start(f32[8,96,256]{2,1,0:T(8,128)S(1)} %collective-permute-done.11), channel_id=1, source_target_pairs={{0,1},{1,0},{2,3},{3,2},{4,5},{5,4},{6,7},{7,6},{8,9},{9,8},{10,11... | collective-permute-start | bytes 2359304 | tf_op jit(solution)/shard_map/ppermute | solution.py:28
  91.4 8.2 %collective-permute-start.15 = (f32[8,96,256]{2,1,0:T(8,128)S(1)}, f32[8,96,256]{2,1,0:T(8,128)S(1)}, u32[]{:S(2)}, u32[]{:S(2)}) collective-permute-start(f32[8,96,256]{2,1,0:T(8,128)S(1)} %collective-permute-done.10), channel_id=1, source_target_pairs={{0,1},{1,0},{2,3},{3,2},{4,5},{5,4},{6,7},{7,6},{8,9},{9,8},{10,11... | collective-permute-start | bytes 2359304 | tf_op jit(solution)/shard_map/ppermute | solution.py:28
  99.3 2.4 %collective-permute-start.17 = (f32[8,96,256]{2,1,0:T(8,128)S(1)}, f32[8,96,256]{2,1,0:T(8,128)S(1)}, u32[]{:S(2)}, u32[]{:S(2)}) collective-permute-start(f32[8,96,256]{2,1,0:T(8,128)S(1)} %constant_dynamic-update-slice_fusion.2), channel_id=1, source_target_pairs={{0,1},{1,0},{2,3},{3,2},{4,5},{5,4},{6,7},{7,6},{8,9},{9,8},{10,11... | collective-permute-start | bytes 2359304 | tf_op jit(solution)/shard_map/ppermute | solution.py:28
  109.9 16.4 %copy-start.12 = (f32[96]{0:T(128)S(1)}, f32[96]{0:T(128)}, u32[]{:S(2)}) copy-start(f32[96]{0:T(128)} %param.22) | copy-start | bytes 1156
  111.4 13.8 %collective-permute-start.19 = (f32[8,8,96]{1,2,0:T(8,128)S(1)}, f32[8,8,96]{1,2,0:T(8,128)S(1)}, u32[]{:S(2)}, u32[]{:S(2)}) collective-permute-start(f32[8,8,96]{1,2,0:T(8,128)S(1)} %get-tuple-element.33), channel_id=1, source_target_pairs={{8,0},{16,8},{24,16},{9,1},{17,9},{25,17},{10,2},{18,10},{26,18},{... | collective-permute-start | bytes 73736 | tf_op jit(solution)/shard_map/ppermute | solution.py:37
  112.7 13.7 %collective-permute-start.18 = (f32[8,8,96]{1,2,0:T(8,128)S(1)}, f32[8,8,96]{1,2,0:T(8,128)S(1)}, u32[]{:S(2)}, u32[]{:S(2)}) collective-permute-start(f32[8,8,96]{1,2,0:T(8,128)S(1)} %get-tuple-element.32), channel_id=1, source_target_pairs={{0,8},{8,16},{16,24},{1,9},{9,17},{17,25},{2,10},{10,18},{18,26},{... | collective-permute-start | bytes 73736 | tf_op jit(solution)/shard_map/ppermute | solution.py:37
  126.8 13.4 %copy-start.4 = (f32[8,96,256]{2,1,0:T(8,128)}, f32[8,96,256]{2,1,0:T(8,128)S(1)}, u32[]{:S(2)}) copy-start(f32[8,96,256]{2,1,0:T(8,128)S(1)} %fusion.40) | copy-start | bytes 2359300
  140.2 16.1 %all-to-all-start.1 = ((f32[8,2,96,128]{3,2,1,0:T(8,128)}), f32[8,2,96,128]{3,2,1,0:T(8,128)S(1)}, u32[]{:S(2)}, u32[]{:S(2)}) async-start(f32[8,2,96,128]{3,2,1,0:T(8,128)} %broadcast_in_dim.123), calls=%async_computation.1 | async-start | bytes 1572864 | tf_op jit(solution)/shard_map/all_to_all | solution.py:20
  158.8 24.5 %all-to-all-start.2 = ((f32[8,2,192,128]{3,2,1,0:T(8,128)}), f32[8,2,192,128]{3,2,1,0:T(8,128)S(1)}, u32[]{:S(2)}, u32[]{:S(2)}) async-start(f32[8,2,192,128]{3,2,1,0:T(8,128)} %broadcast_in_dim.125), calls=%async_computation.2 | async-start | bytes 3145728 | tf_op jit(solution)/shard_map/all_to_all | solution.py:20
  194.2 34.6 %copy-start.1 = (f32[5,96,768]{2,1,0:T(8,128)S(1)}, f32[5,96,768]{2,1,0:T(8,128)}, u32[]{:S(2)}) copy-start(f32[5,96,768]{2,1,0:T(8,128)} %param.19) | copy-start | bytes 4423684
  (6 other events, 32.3 us)

commit v4 on v3

--- a/solution.py
+++ b/solution.py
@@ -168,8 +168,8 @@
     head_result = weighted_values / denominator[..., None]
     out_width = out_weight.shape[1] // group
     out_blocks = out_weight.reshape(out_weight.shape[0], group, out_width)
-    shares = jnp.einsum("btd,dne->nbte", head_result, out_blocks, precision=MATMUL_PRECISION)
-    summed = jnp.sum(lax.all_to_all(shares, CHANNELS, 0, 0, tiled=True), axis=0)
+    shares = jnp.einsum("btd,dne->nbet", head_result, out_blocks, precision=MATMUL_PRECISION)
+    summed = jnp.swapaxes(jnp.sum(lax.all_to_all(shares, CHANNELS, 0, 0, tiled=True), axis=0), 1, 2)
     by_block = jnp.transpose(summed.reshape(per, seq, pooled_rows, out_width), (1, 0, 2, 3))
     back = lax.all_to_all(packed(by_block), "seq", 0, 0, tiled=True)
     return unpacked(back, pooled_rows, out_width).reshape(batch_count, pooled_rows, out_width)

time: 229 us -> 229 us (level)
  no operation moved by 1% of the time
where the time goes in v4:
time: 229 us
  waiting for transfers between devices  92.7 us (40%)
  blocking collectives  44.9 us (20%)
  starting transfers between devices  32.2 us (14%)
  matrix products  20.1 us (9%)
  local copies, waits for them, and re-layouts  19.6 us (9%)
  other arithmetic  18.1 us (8%)
    ppermute x2, waiting for transfers between devices, row_exchange(): across = lax.ppermute(activated, 'crow', pairs(1))  33 us
    all_to_all x2, waiting for transfers between devices, gathered(): return lax.all_to_all(copies, axis_name, 0, 0, tiled=True)  24.7 us
    all_to_all x1, blocking collectives, attention_by_batch(): lax.all_to_all(shares, CHANNELS, 0, 0, tiled=True)  23.5 us
    ppermute x4, waiting for transfers between devices, shifted_in(): return lax.ppermute(edge, 'seq', pairs)  16.9 us
    ppermute x4, starting transfers between devices, shifted_in(): return lax.ppermute(edge, 'seq', pairs)  12.4 us
    ppermute x2, waiting for transfers between devices, row_exchange(): first = lax.ppermute(across[:half], 'crow', pairs(2))  11.7 us
    all_to_all x1, blocking collectives, attention_by_batch(): lax.all_to_all(pooled.reshape(seq, per, pooled_rows, channels), 'seq', 0,...  11.7 us
    dot_general x2, matrix products, convolution_block(): jnp.einsum('btc,koc->kbto', ordered, kernel, precision=MATMUL_PRECISION)  10.9 us
  transfers between devices with their start and end apart: 22, of which 14 were waited for; matrix products, arithmetic and copies ran while one was open for 6% of the time, Pallas kernels for 0%

profile of v4, /device:TPU:0, one launch (start us, length us, event | category | flops | bytes accessed | tf_op | source)
XLA Modules:
  0.0 228.8 jit_solution(11215904428517466731)
XLA Ops:
  0.7 4.0 %fusion.36 = f32[8,96,256]{2,1,0:T(8,128)} fusion(f32[8,96,256]{2,1,0:T(8,128)} %param.15, f32[96]{0:T(128)} %param.17, f32[96]{0:T(128)} %param.16), kind=kLoop, calls=%fused_computation.55 | loop fusion | flops 12976128 | bytes 1573632 | tf_op jit(solution)/shard_map/mul | solution.py:53
  4.6 2.9 %collective-permute-start = (f32[8,96,256]{2,1,0:T(8,128)}, f32[8,96,256]{2,1,0:T(8,128)S(1)}, u32[]{:S(2)}, u32[]{:S(2)}) collective-permute-start(f32[8,96,256]{2,1,0:T(8,128)} %fusion.36), channel_id=1, source_target_pairs={{0,2},{2,0},{4,6},{6,4},{1,3},{3,1},{5,7},{7,5},{8,10},{10,8},{12,... | collective-permute-start | bytes 2359304 | tf_op jit(solution)/shard_map/ppermute | solution.py:42
  7.6 1.5 collective-permute-start.1
  9.1 16.2 %collective-permute-done = f32[8,96,256]{2,1,0:T(8,128)S(1)} collective-permute-done((f32[8,96,256]{2,1,0:T(8,128)}, f32[8,96,256]{2,1,0:T(8,128)S(1)}, u32[]{:S(2)}, u32[]{:S(2)}) %collective-permute-start) | collective-permute-done | bytes 786464 | tf_op jit(solution)/shard_map/ppermute | solution.py:42
  26.1 1.8 collective-permute-start.2
  29.6 1.5 collective-permute-start.3
  31.9 4.8 %collective-permute-done.2 = f32[4,96,256]{2,1,0:T(8,128)S(1)} collective-permute-done((f32[4,96,256]{2,1,0:T(8,128)}, f32[4,96,256]{2,1,0:T(8,128)S(1)}, u32[]{:S(2)}, u32[]{:S(2)}) %collective-permute-start.2) | collective-permute-done | bytes 393248 | tf_op jit(solution)/shard_map/ppermute | solution.py:45
  36.7 2.9 %collective-permute-done.3 = f32[4,96,256]{2,1,0:T(8,128)} collective-permute-done((f32[4,96,256]{2,1,0:T(8,128)}, f32[4,96,256]{2,1,0:T(8,128)}, u32[]{:S(2)}, u32[]{:S(2)}) %collective-permute-start.3) | collective-permute-done | bytes 393248 | tf_op jit(solution)/shard_map/ppermute | solution.py:46
  40.7 1.8 fusion.76
  46.1 5.5 %fusion.10 = f32[5,8,256,96]{2,3,0,1:T(8,128)S(1)} fusion(f32[8,256,768]{1,2,0:T(8,128)S(1)} %bitcast_select_fusion.1, f32[5,96,768]{2,1,0:T(8,128)S(1)} %copy-done), kind=kOutput, calls=%fused_computation.28 | convolution fusion | flops 4529848320 | bytes 11698176 | tf_op jit(solution)/shard_map/btc,koc->kbto/dot_general | solution.py:68
  51.7 1.5 fusion.25
  54.6 4.6 %collective-permute-start.8 = (f32[8,4,96]{1,2,0:T(8,128)S(1)}, f32[8,4,96]{1,2,0:T(8,128)S(1)}, u32[]{:S(2)}, u32[]{:S(2)}) collective-permute-start(f32[8,4,96]{1,2,0:T(8,128)S(1)} %get-tuple-element.34), channel_id=1, source_target_pairs={{0,8},{8,16},{16,24},{1,9},{9,17},{17,25},{2,10},{10,18},{18,26},{... | collective-permute-start | bytes 36872 | tf_op jit(solution)/shard_map/ppermute | solution.py:37
  59.3 7.4 %collective-permute-done.9 = f32[8,4,96]{1,2,0:T(8,128)S(1)} collective-permute-done((f32[8,4,96]{1,2,0:T(8,128)S(1)}, f32[8,4,96]{1,2,0:T(8,128)S(1)}, u32[]{:S(2)}, u32[]{:S(2)}) %collective-permute-start.9) | collective-permute-done | bytes 12320 | tf_op jit(solution)/shard_map/ppermute | solution.py:37
  67.9 2.0 fusion.38
  69.9 1.6 collective-permute-start.10
  71.9 16.8 %collective-permute-done.10 = f32[8,96,256]{2,1,0:T(8,128)S(1)} collective-permute-done((f32[8,96,256]{2,1,0:T(8,128)S(1)}, f32[8,96,256]{2,1,0:T(8,128)S(1)}, u32[]{:S(2)}, u32[]{:S(2)}) %collective-permute-start.10) | collective-permute-done | bytes 786464 | tf_op jit(solution)/shard_map/ppermute | solution.py:42
  91.4 6.9 %collective-permute-done.12 = f32[4,96,256]{2,1,0:T(8,128)S(1)} collective-permute-done((f32[4,96,256]{2,1,0:T(8,128)S(1)}, f32[4,96,256]{2,1,0:T(8,128)S(1)}, u32[]{:S(2)}, u32[]{:S(2)}) %collective-permute-start.12) | collective-permute-done | bytes 393248 | tf_op jit(solution)/shard_map/ppermute | solution.py:45
  99.7 2.0 collective-permute-done.17
  104.5 5.4 %fusion.7 = f32[5,8,256,96]{2,3,1,0:T(8,128)S(1)} fusion(f32[8,256,768]{1,2,0:T(8,128)S(1)} %bitcast_select_fusion, f32[5,96,768]{2,1,0:T(8,128)S(1)} %copy-done.7), kind=kOutput, calls=%fused_computation.27 | convolution fusion | flops 4529848320 | bytes 11698176 | tf_op jit(solution)/shard_map/btc,koc->kbto/dot_general | solution.py:68
  112.7 5.3 %collective-permute-start.18 = (f32[8,8,96]{1,2,0:T(8,128)S(1)}, f32[8,8,96]{1,2,0:T(8,128)S(1)}, u32[]{:S(2)}, u32[]{:S(2)}) collective-permute-start(f32[8,8,96]{1,2,0:T(8,128)S(1)} %get-tuple-element.32), channel_id=1, source_target_pairs={{0,8},{8,16},{16,24},{1,9},{9,17},{17,25},{2,10},{10,18},{18,26},{... | collective-permute-start | bytes 73736 | tf_op jit(solution)/shard_map/ppermute | solution.py:37
  118.0 7.1 %collective-permute-done.19 = f32[8,8,96]{1,2,0:T(8,128)S(1)} collective-permute-done((f32[8,8,96]{1,2,0:T(8,128)S(1)}, f32[8,8,96]{1,2,0:T(8,128)S(1)}, u32[]{:S(2)}, u32[]{:S(2)}) %collective-permute-start.19) | collective-permute-done | bytes 24608 | tf_op jit(solution)/shard_map/ppermute | solution.py:37
  127.4 11.7 %all_to_all.25 = f32[4,2,32,96]{3,2,1,0:T(8,128)S(1)} all-to-all(f32[4,2,32,96]{3,2,1,0:T(8,128)S(1)} %bitcast.165), channel_id=1, replica_groups=mesh['seq'=4,'crow'=4,'ccol'=2] {'seq'}, dimensions={0} | all-to-all | bytes 196608 | tf_op jit(solution)/shard_map/all_to_all | solution.py:151
  140.2 3.5 %all-to-all-start.1 = ((f32[8,2,96,128]{3,2,1,0:T(8,128)}), f32[8,2,96,128]{3,2,1,0:T(8,128)S(1)}, u32[]{:S(2)}, u32[]{:S(2)}) async-start(f32[8,2,96,128]{3,2,1,0:T(8,128)} %broadcast_in_dim.123), calls=%async_computation.1 | async-start | bytes 1572864 | tf_op jit(solution)/shard_map/all_to_all | solution.py:20
  145.2 11.1 %all-to-all-done.1 = f32[8,2,96,128]{3,2,1,0:T(8,128)S(1)} async-done(((f32[8,2,96,128]{3,2,1,0:T(8,128)}), f32[8,2,96,128]{3,2,1,0:T(8,128)S(1)}, u32[]{:S(2)}, u32[]{:S(2)}) %all-to-all-start.1) | async-done | bytes 786464 | tf_op jit(solution)/shard_map/all_to_all | solution.py:20
  158.8 3.6 %all-to-all-start.2 = ((f32[8,2,192,128]{3,2,1,0:T(8,128)}), f32[8,2,192,128]{3,2,1,0:T(8,128)S(1)}, u32[]{:S(2)}, u32[]{:S(2)}) async-start(f32[8,2,192,128]{3,2,1,0:T(8,128)} %broadcast_in_dim.125), calls=%async_computation.2 | async-start | bytes 3145728 | tf_op jit(solution)/shard_map/all_to_all | solution.py:20
  162.4 5.4 %copy.65 = f32[1536,576]{1,0:T(8,128)} copy(f32[1536,576]{0,1:T(8,128)} %param.26) | data formatting | bytes 7077888 | tf_op args[11]
  167.9 1.6 copy.89
  169.8 13.6 %all-to-all-done.2 = f32[8,2,192,128]{3,2,1,0:T(8,128)S(1)} async-done(((f32[8,2,192,128]{3,2,1,0:T(8,128)}), f32[8,2,192,128]{3,2,1,0:T(8,128)S(1)}, u32[]{:S(2)}, u32[]{:S(2)}) %all-to-all-start.2) | async-done | bytes 1572896 | tf_op jit(solution)/shard_map/all_to_all | solution.py:20
  183.7 1.8 reshape.144
  185.5 6.9 %fusion.18 = f32[2,128,576]{1,2,0:T(8,128)S(1)} fusion(f32[8,192,576,1]{2,1,3,0:T(8,128)} %bitcast.146, f32[8,2,128,192]{3,2,1,0:T(8,128)} %reshape.144, f32[8,192]{1,0:T(8,128)S(1)} %mul.194, f32[2,128]{1,0:T(2,128)S(1)} %add_sqrt_fusion), kind=kOutput, calls=%fused_computation.34 | convolution fusion | flops 1359495168 | bytes 5708800 | tf_op jit(solution)/shard_map/nbtj,njo->bto/dot_general | solution.py:134
  194.3 23.5 %all_to_all.26 = f32[8,2,192,128]{3,2,1,0:T(8,128)S(1)} all-to-all(f32[8,2,192,128]{3,2,1,0:T(8,128)S(1)} %copy.69), channel_id=1, replica_groups=mesh['seq'=4,'crow'=4,'ccol'=2] {'crow','ccol'}, dimensions={0} | all-to-all | bytes 3145728 | tf_op jit(solution)/shard_map/all_to_all | solution.py:172
  218.3 9.7 %all_to_all.27 = f32[4,2,48,128]{3,2,1,0:T(8,128)S(1)} all-to-all(f32[4,2,48,128]{3,2,1,0:T(8,128)S(1)} %copy.72), channel_id=1, replica_groups=mesh['seq'=4,'crow'=4,'ccol'=2] {'seq'}, dimensions={0} | all-to-all | bytes 393216 | tf_op jit(solution)/shard_map/all_to_all | solution.py:174
  (116 shorter events, 31.6 us)
Async XLA Ops:
  0.6 45.5 %copy-start = (f32[5,96,768]{2,1,0:T(8,128)S(1)}, f32[5,96,768]{2,1,0:T(8,128)}, u32[]{:S(2)}) copy-start(f32[5,96,768]{2,1,0:T(8,128)} %param.19) | copy-start | bytes 4423684
  0.6 40.1 %copy-start.2 = (f32[8,96,256]{2,1,0:T(8,128)S(1)}, f32[8,96,256]{2,1,0:T(8,128)}, u32[]{:S(2)}) copy-start(f32[8,96,256]{2,1,0:T(8,128)} %param.15) | copy-start | bytes 2359300
  0.7 40.1 %copy-start.10 = (f32[96]{0:T(128)S(1)}, f32[96]{0:T(128)}, u32[]{:S(2)}) copy-start(f32[96]{0:T(128)} %param.17) | copy-start | bytes 1156
  0.7 40.1 %copy-start.11 = (f32[96]{0:T(128)S(1)}, f32[96]{0:T(128)}, u32[]{:S(2)}) copy-start(f32[96]{0:T(128)} %param.16) | copy-start | bytes 1156
  4.6 20.7 %collective-permute-start = (f32[8,96,256]{2,1,0:T(8,128)}, f32[8,96,256]{2,1,0:T(8,128)S(1)}, u32[]{:S(2)}, u32[]{:S(2)}) collective-permute-start(f32[8,96,256]{2,1,0:T(8,128)} %fusion.36), channel_id=1, source_target_pairs={{0,2},{2,0},{4,6},{6,4},{1,3},{3,1},{5,7},{7,5},{8,10},{10,8},{12,... | collective-permute-start | bytes 2359304 | tf_op jit(solution)/shard_map/ppermute | solution.py:42
  7.6 20.3 %collective-permute-start.1 = (f32[8,96,256]{2,1,0:T(8,128)}, f32[8,96,256]{2,1,0:T(8,128)S(1)}, u32[]{:S(2)}, u32[]{:S(2)}) collective-permute-start(f32[8,96,256]{2,1,0:T(8,128)} %fusion.36), channel_id=1, source_target_pairs={{0,4},{2,6},{4,0},{6,2},{1,5},{3,7},{5,1},{7,3},{8,12},{10,14},{12... | collective-permute-start | bytes 2359304 | tf_op jit(solution)/shard_map/ppermute | solution.py:43
  26.1 10.5 %collective-permute-start.2 = (f32[4,96,256]{2,1,0:T(8,128)}, f32[4,96,256]{2,1,0:T(8,128)S(1)}, u32[]{:S(2)}, u32[]{:S(2)}) collective-permute-start(f32[4,96,256]{2,1,0:T(8,128)} %slice.117), channel_id=1, source_target_pairs={{0,4},{2,6},{4,0},{6,2},{1,5},{3,7},{5,1},{7,3},{8,12},{10,14},{12... | collective-permute-start | bytes 1179656 | tf_op jit(solution)/shard_map/ppermute | solution.py:45
  29.6 10.0 %collective-permute-start.3 = (f32[4,96,256]{2,1,0:T(8,128)}, f32[4,96,256]{2,1,0:T(8,128)}, u32[]{:S(2)}, u32[]{:S(2)}) collective-permute-start(f32[4,96,256]{2,1,0:T(8,128)} %slice.118), channel_id=1, source_target_pairs={{0,2},{2,0},{4,6},{6,4},{1,3},{3,1},{5,7},{7,5},{8,10},{10,8},{12,... | collective-permute-start | bytes 1179656 | tf_op jit(solution)/shard_map/ppermute | solution.py:46
  31.1 12.1 %collective-permute-start.4 = (f32[8,96,256]{2,1,0:T(8,128)}, f32[8,96,256]{2,1,0:T(8,128)}, u32[]{:S(2)}, u32[]{:S(2)}) collective-permute-start(f32[8,96,256]{2,1,0:T(8,128)} %fusion.36), channel_id=1, source_target_pairs={{0,1},{1,0},{2,3},{3,2},{4,5},{5,4},{6,7},{7,6},{8,9},{9,8},{10,11... | collective-permute-start | bytes 2359304 | tf_op jit(solution)/shard_map/ppermute | solution.py:28
  31.2 11.9 %collective-permute-start.6 = (f32[8,96,256]{2,1,0:T(8,128)}, f32[8,96,256]{2,1,0:T(8,128)S(1)}, u32[]{:S(2)}, u32[]{:S(2)}) collective-permute-start(f32[8,96,256]{2,1,0:T(8,128)} %copy-done.5), channel_id=1, source_target_pairs={{0,1},{1,0},{2,3},{3,2},{4,5},{5,4},{6,7},{7,6},{8,9},{9,8},{10,11... | collective-permute-start | bytes 2359304 | tf_op jit(solution)/shard_map/ppermute | solution.py:28
  31.8 11.4 %collective-permute-start.5 = (f32[8,96,256]{2,1,0:T(8,128)S(1)}, f32[8,96,256]{2,1,0:T(8,128)S(1)}, u32[]{:S(2)}, u32[]{:S(2)}) collective-permute-start(f32[8,96,256]{2,1,0:T(8,128)S(1)} %collective-permute-done), channel_id=1, source_target_pairs={{0,1},{1,0},{2,3},{3,2},{4,5},{5,4},{6,7},{7,6},{8,9},{9,8},{10,11... | collective-permute-start | bytes 2359304 | tf_op jit(solution)/shard_map/ppermute | solution.py:28
  40.6 2.5 %collective-permute-start.7 = (f32[8,96,256]{2,1,0:T(8,128)S(1)}, f32[8,96,256]{2,1,0:T(8,128)S(1)}, u32[]{:S(2)}, u32[]{:S(2)}) collective-permute-start(f32[8,96,256]{2,1,0:T(8,128)S(1)} %constant_dynamic-update-slice_fusion), channel_id=1, source_target_pairs={{0,1},{1,0},{2,3},{3,2},{4,5},{5,4},{6,7},{7,6},{8,9},{9,8},{10,11... | collective-permute-start | bytes 2359304 | tf_op jit(solution)/shard_map/ppermute | solution.py:28
  51.6 16.2 %copy-start.13 = (f32[96]{0:T(128)S(1)}, f32[96]{0:T(128)}, u32[]{:S(2)}) copy-start(f32[96]{0:T(128)} %param.21) | copy-start | bytes 1156
  51.7 16.2 %copy-start.14 = (f32[96]{0:T(128)S(1)}, f32[96]{0:T(128)}, u32[]{:S(2)}) copy-start(f32[96]{0:T(128)} %param.20) | copy-start | bytes 1156
  51.7 16.2 %copy-start.15 = (f32[96]{0:T(128)S(1)}, f32[96]{0:T(128)}, u32[]{:S(2)}) copy-start(f32[96]{0:T(128)} %param.18) | copy-start | bytes 1156
  53.3 13.4 %collective-permute-start.9 = (f32[8,4,96]{1,2,0:T(8,128)S(1)}, f32[8,4,96]{1,2,0:T(8,128)S(1)}, u32[]{:S(2)}, u32[]{:S(2)}) collective-permute-start(f32[8,4,96]{1,2,0:T(8,128)S(1)} %get-tuple-element.35), channel_id=1, source_target_pairs={{8,0},{16,8},{24,16},{9,1},{17,9},{25,17},{10,2},{18,10},{26,18},{... | collective-permute-start | bytes 36872 | tf_op jit(solution)/shard_map/ppermute | solution.py:37
  54.6 13.3 %collective-permute-start.8 = (f32[8,4,96]{1,2,0:T(8,128)S(1)}, f32[8,4,96]{1,2,0:T(8,128)S(1)}, u32[]{:S(2)}, u32[]{:S(2)}) collective-permute-start(f32[8,4,96]{1,2,0:T(8,128)S(1)} %get-tuple-element.34), channel_id=1, source_target_pairs={{0,8},{8,16},{16,24},{1,9},{9,17},{17,25},{2,10},{10,18},{18,26},{... | collective-permute-start | bytes 36872 | tf_op jit(solution)/shard_map/ppermute | solution.py:37
  69.9 18.9 %collective-permute-start.10 = (f32[8,96,256]{2,1,0:T(8,128)S(1)}, f32[8,96,256]{2,1,0:T(8,128)S(1)}, u32[]{:S(2)}, u32[]{:S(2)}) collective-permute-start(f32[8,96,256]{2,1,0:T(8,128)S(1)} %get-tuple-element.14), channel_id=1, source_target_pairs={{0,2},{2,0},{4,6},{6,4},{1,3},{3,1},{5,7},{7,5},{8,10},{10,8},{12,... | collective-permute-start | bytes 2359304 | tf_op jit(solution)/shard_map/ppermute | solution.py:42
  71.4 18.6 %collective-permute-start.11 = (f32[8,96,256]{2,1,0:T(8,128)S(1)}, f32[8,96,256]{2,1,0:T(8,128)S(1)}, u32[]{:S(2)}, u32[]{:S(2)}) collective-permute-start(f32[8,96,256]{2,1,0:T(8,128)S(1)} %get-tuple-element.14), channel_id=1, source_target_pairs={{0,4},{2,6},{4,0},{6,2},{1,5},{3,7},{5,1},{7,3},{8,12},{10,14},{12... | collective-permute-start | bytes 2359304 | tf_op jit(solution)/shard_map/ppermute | solution.py:43
  88.8 9.6 %collective-permute-start.12 = (f32[4,96,256]{2,1,0:T(8,128)S(1)}, f32[4,96,256]{2,1,0:T(8,128)S(1)}, u32[]{:S(2)}, u32[]{:S(2)}) collective-permute-start(f32[4,96,256]{2,1,0:T(8,128)S(1)} %slice.122), channel_id=1, source_target_pairs={{0,4},{2,6},{4,0},{6,2},{1,5},{3,7},{5,1},{7,3},{8,12},{10,14},{12... | collective-permute-start | bytes 1179656 | tf_op jit(solution)/shard_map/ppermute | solution.py:45
  90.0 9.2 %collective-permute-start.13 = (f32[4,96,256]{2,1,0:T(8,128)S(1)}, f32[4,96,256]{2,1,0:T(8,128)S(1)}, u32[]{:S(2)}, u32[]{:S(2)}) collective-permute-start(f32[4,96,256]{2,1,0:T(8,128)S(1)} %slice.123), channel_id=1, source_target_pairs={{0,2},{2,0},{4,6},{6,4},{1,3},{3,1},{5,7},{7,5},{8,10},{10,8},{12,... | collective-permute-start | bytes 1179656 | tf_op jit(solution)/shard_map/ppermute | solution.py:46
  90.9 8.7 %collective-permute-start.14 = (f32[8,96,256]{2,1,0:T(8,128)S(1)}, f32[8,96,256]{2,1,0:T(8,128)S(1)}, u32[]{:S(2)}, u32[]{:S(2)}) collective-permute-start(f32[8,96,256]{2,1,0:T(8,128)S(1)} %get-tuple-element.14), channel_id=1, source_target_pairs={{0,1},{1,0},{2,3},{3,2},{4,5},{5,4},{6,7},{7,6},{8,9},{9,8},{10,11... | collective-permute-start | bytes 2359304 | tf_op jit(solution)/shard_map/ppermute | solution.py:28
  90.9 8.7 %collective-permute-start.16 = (f32[8,96,256]{2,1,0:T(8,128)S(1)}, f32[8,96,256]{2,1,0:T(8,128)S(1)}, u32[]{:S(2)}, u32[]{:S(2)}) collective-permute-start(f32[8,96,256]{2,1,0:T(8,128)S(1)} %collective-permute-done.11), channel_id=1, source_target_pairs={{0,1},{1,0},{2,3},{3,2},{4,5},{5,4},{6,7},{7,6},{8,9},{9,8},{10,11... | collective-permute-start | bytes 2359304 | tf_op jit(solution)/shard_map/ppermute | solution.py:28
  91.4 8.2 %collective-permute-start.15 = (f32[8,96,256]{2,1,0:T(8,128)S(1)}, f32[8,96,256]{2,1,0:T(8,128)S(1)}, u32[]{:S(2)}, u32[]{:S(2)}) collective-permute-start(f32[8,96,256]{2,1,0:T(8,128)S(1)} %collective-permute-done.10), channel_id=1, source_target_pairs={{0,1},{1,0},{2,3},{3,2},{4,5},{5,4},{6,7},{7,6},{8,9},{9,8},{10,11... | collective-permute-start | bytes 2359304 | tf_op jit(solution)/shard_map/ppermute | solution.py:28
  99.3 2.4 %collective-permute-start.17 = (f32[8,96,256]{2,1,0:T(8,128)S(1)}, f32[8,96,256]{2,1,0:T(8,128)S(1)}, u32[]{:S(2)}, u32[]{:S(2)}) collective-permute-start(f32[8,96,256]{2,1,0:T(8,128)S(1)} %constant_dynamic-update-slice_fusion.2), channel_id=1, source_target_pairs={{0,1},{1,0},{2,3},{3,2},{4,5},{5,4},{6,7},{7,6},{8,9},{9,8},{10,11... | collective-permute-start | bytes 2359304 | tf_op jit(solution)/shard_map/ppermute | solution.py:28
  109.9 16.4 %copy-start.12 = (f32[96]{0:T(128)S(1)}, f32[96]{0:T(128)}, u32[]{:S(2)}) copy-start(f32[96]{0:T(128)} %param.22) | copy-start | bytes 1156
  111.4 13.8 %collective-permute-start.19 = (f32[8,8,96]{1,2,0:T(8,128)S(1)}, f32[8,8,96]{1,2,0:T(8,128)S(1)}, u32[]{:S(2)}, u32[]{:S(2)}) collective-permute-start(f32[8,8,96]{1,2,0:T(8,128)S(1)} %get-tuple-element.33), channel_id=1, source_target_pairs={{8,0},{16,8},{24,16},{9,1},{17,9},{25,17},{10,2},{18,10},{26,18},{... | collective-permute-start | bytes 73736 | tf_op jit(solution)/shard_map/ppermute | solution.py:37
  112.7 13.7 %collective-permute-start.18 = (f32[8,8,96]{1,2,0:T(8,128)S(1)}, f32[8,8,96]{1,2,0:T(8,128)S(1)}, u32[]{:S(2)}, u32[]{:S(2)}) collective-permute-start(f32[8,8,96]{1,2,0:T(8,128)S(1)} %get-tuple-element.32), channel_id=1, source_target_pairs={{0,8},{8,16},{16,24},{1,9},{9,17},{17,25},{2,10},{10,18},{18,26},{... | collective-permute-start | bytes 73736 | tf_op jit(solution)/shard_map/ppermute | solution.py:37
  126.8 13.4 %copy-start.4 = (f32[8,96,256]{2,1,0:T(8,128)}, f32[8,96,256]{2,1,0:T(8,128)S(1)}, u32[]{:S(2)}) copy-start(f32[8,96,256]{2,1,0:T(8,128)S(1)} %fusion.40) | copy-start | bytes 2359300
  140.2 16.1 %all-to-all-start.1 = ((f32[8,2,96,128]{3,2,1,0:T(8,128)}), f32[8,2,96,128]{3,2,1,0:T(8,128)S(1)}, u32[]{:S(2)}, u32[]{:S(2)}) async-start(f32[8,2,96,128]{3,2,1,0:T(8,128)} %broadcast_in_dim.123), calls=%async_computation.1 | async-start | bytes 1572864 | tf_op jit(solution)/shard_map/all_to_all | solution.py:20
  158.8 24.5 %all-to-all-start.2 = ((f32[8,2,192,128]{3,2,1,0:T(8,128)}), f32[8,2,192,128]{3,2,1,0:T(8,128)S(1)}, u32[]{:S(2)}, u32[]{:S(2)}) async-start(f32[8,2,192,128]{3,2,1,0:T(8,128)} %broadcast_in_dim.125), calls=%async_computation.2 | async-start | bytes 3145728 | tf_op jit(solution)/shard_map/all_to_all | solution.py:20
  194.2 34.6 %copy-start.1 = (f32[5,96,768]{2,1,0:T(8,128)S(1)}, f32[5,96,768]{2,1,0:T(8,128)}, u32[]{:S(2)}) copy-start(f32[5,96,768]{2,1,0:T(8,128)} %param.19) | copy-start | bytes 4423684
  (6 other events, 32.3 us)

commit v5 on v3

--- a/solution.py
+++ b/solution.py
@@ -150,7 +150,7 @@
     length = seq * pooled_rows
     mine = lax.all_to_all(pooled.reshape(seq, per, pooled_rows, channels), "seq", 0, 0, tiled=True)
     mine = jnp.transpose(mine, (1, 0, 2, 3)).reshape(per, length, channels)
-    pooled_all = gathered_packed(mine, CHANNELS)
+    pooled_all = gathered(mine, CHANNELS)
     up_blocks = up_weight.reshape(up_weight.shape[0], group, channels)
     hidden = jnp.einsum("nbti,oni->bto", pooled_all, up_blocks, precision=MATMUL_PRECISION)
     hidden_all = gathered_packed(hidden, CHANNELS)

time: 229 us -> 229 us (level)
  no operation moved by 1% of the time
where the time goes in v5:
time: 229 us
  waiting for transfers between devices  92.6 us (40%)
  blocking collectives  44.9 us (20%)
  starting transfers between devices  32.2 us (14%)
  matrix products  20.3 us (9%)
  local copies, waits for them, and re-layouts  19.3 us (8%)
  other arithmetic  18.1 us (8%)
    ppermute x2, waiting for transfers between devices, row_exchange(): across = lax.ppermute(activated, 'crow', pairs(1))  33 us
    all_to_all x2, waiting for transfers between devices, gathered(): return lax.all_to_all(copies, axis_name, 0, 0, tiled=True)  24.6 us
    all_to_all x1, blocking collectives, attention_by_batch(): summed = jnp.sum(lax.all_to_all(shares, CHANNELS, 0, 0, tiled=True), axis=0)  23.5 us
    ppermute x4, waiting for transfers between devices, shifted_in(): return lax.ppermute(edge, 'seq', pairs)  16.9 us
    ppermute x4, starting transfers between devices, shifted_in(): return lax.ppermute(edge, 'seq', pairs)  12.4 us
    ppermute x2, waiting for transfers between devices, row_exchange(): first = lax.ppermute(across[:half], 'crow', pairs(2))  11.7 us
    all_to_all x1, blocking collectives, attention_by_batch(): lax.all_to_all(pooled.reshape(seq, per, pooled_rows, channels), 'seq', 0,...  11.7 us
    dot_general x2, matrix products, convolution_block(): jnp.einsum('btc,koc->kbto', ordered, kernel, precision=MATMUL_PRECISION)  10.9 us
  transfers between devices with their start and end apart: 22, of which 14 were waited for; matrix products, arithmetic and copies ran while one was open for 6% of the time, Pallas kernels for 0%

profile of v5, /device:TPU:0, one launch (start us, length us, event | category | flops | bytes accessed | tf_op | source)
XLA Modules:
  0.0 228.7 jit_solution(16910246432839533128)
XLA Ops:
  0.7 4.0 %fusion.36 = f32[8,96,256]{2,1,0:T(8,128)} fusion(f32[8,96,256]{2,1,0:T(8,128)} %param.15, f32[96]{0:T(128)} %param.17, f32[96]{0:T(128)} %param.16), kind=kLoop, calls=%fused_computation.55 | loop fusion | flops 12976128 | bytes 1573632 | tf_op jit(solution)/shard_map/mul | solution.py:53
  4.6 2.9 %collective-permute-start = (f32[8,96,256]{2,1,0:T(8,128)}, f32[8,96,256]{2,1,0:T(8,128)S(1)}, u32[]{:S(2)}, u32[]{:S(2)}) collective-permute-start(f32[8,96,256]{2,1,0:T(8,128)} %fusion.36), channel_id=1, source_target_pairs={{0,2},{2,0},{4,6},{6,4},{1,3},{3,1},{5,7},{7,5},{8,10},{10,8},{12,... | collective-permute-start | bytes 2359304 | tf_op jit(solution)/shard_map/ppermute | solution.py:42
  7.6 1.5 collective-permute-start.1
  9.1 16.2 %collective-permute-done = f32[8,96,256]{2,1,0:T(8,128)S(1)} collective-permute-done((f32[8,96,256]{2,1,0:T(8,128)}, f32[8,96,256]{2,1,0:T(8,128)S(1)}, u32[]{:S(2)}, u32[]{:S(2)}) %collective-permute-start) | collective-permute-done | bytes 786464 | tf_op jit(solution)/shard_map/ppermute | solution.py:42
  26.1 1.8 collective-permute-start.2
  29.6 1.5 collective-permute-start.3
  31.9 4.8 %collective-permute-done.2 = f32[4,96,256]{2,1,0:T(8,128)S(1)} collective-permute-done((f32[4,96,256]{2,1,0:T(8,128)}, f32[4,96,256]{2,1,0:T(8,128)S(1)}, u32[]{:S(2)}, u32[]{:S(2)}) %collective-permute-start.2) | collective-permute-done | bytes 393248 | tf_op jit(solution)/shard_map/ppermute | solution.py:45
  36.7 2.9 %collective-permute-done.3 = f32[4,96,256]{2,1,0:T(8,128)} collective-permute-done((f32[4,96,256]{2,1,0:T(8,128)}, f32[4,96,256]{2,1,0:T(8,128)}, u32[]{:S(2)}, u32[]{:S(2)}) %collective-permute-start.3) | collective-permute-done | bytes 393248 | tf_op jit(solution)/shard_map/ppermute | solution.py:46
  40.7 1.8 fusion.76
  46.1 5.5 %fusion.10 = f32[5,8,256,96]{2,3,0,1:T(8,128)S(1)} fusion(f32[8,256,768]{1,2,0:T(8,128)S(1)} %bitcast_select_fusion.1, f32[5,96,768]{2,1,0:T(8,128)S(1)} %copy-done), kind=kOutput, calls=%fused_computation.28 | convolution fusion | flops 4529848320 | bytes 11698176 | tf_op jit(solution)/shard_map/btc,koc->kbto/dot_general | solution.py:68
  51.7 1.5 fusion.25
  54.6 4.6 %collective-permute-start.8 = (f32[8,4,96]{1,2,0:T(8,128)S(1)}, f32[8,4,96]{1,2,0:T(8,128)S(1)}, u32[]{:S(2)}, u32[]{:S(2)}) collective-permute-start(f32[8,4,96]{1,2,0:T(8,128)S(1)} %get-tuple-element.34), channel_id=1, source_target_pairs={{0,8},{8,16},{16,24},{1,9},{9,17},{17,25},{2,10},{10,18},{18,26},{... | collective-permute-start | bytes 36872 | tf_op jit(solution)/shard_map/ppermute | solution.py:37
  59.3 7.4 %collective-permute-done.9 = f32[8,4,96]{1,2,0:T(8,128)S(1)} collective-permute-done((f32[8,4,96]{1,2,0:T(8,128)S(1)}, f32[8,4,96]{1,2,0:T(8,128)S(1)}, u32[]{:S(2)}, u32[]{:S(2)}) %collective-permute-start.9) | collective-permute-done | bytes 12320 | tf_op jit(solution)/shard_map/ppermute | solution.py:37
  67.9 2.0 fusion.38
  69.9 1.6 collective-permute-start.10
  71.9 16.8 %collective-permute-done.10 = f32[8,96,256]{2,1,0:T(8,128)S(1)} collective-permute-done((f32[8,96,256]{2,1,0:T(8,128)S(1)}, f32[8,96,256]{2,1,0:T(8,128)S(1)}, u32[]{:S(2)}, u32[]{:S(2)}) %collective-permute-start.10) | collective-permute-done | bytes 786464 | tf_op jit(solution)/shard_map/ppermute | solution.py:42
  91.4 6.9 %collective-permute-done.12 = f32[4,96,256]{2,1,0:T(8,128)S(1)} collective-permute-done((f32[4,96,256]{2,1,0:T(8,128)S(1)}, f32[4,96,256]{2,1,0:T(8,128)S(1)}, u32[]{:S(2)}, u32[]{:S(2)}) %collective-permute-start.12) | collective-permute-done | bytes 393248 | tf_op jit(solution)/shard_map/ppermute | solution.py:45
  99.7 2.0 collective-permute-done.17
  104.5 5.4 %fusion.7 = f32[5,8,256,96]{2,3,1,0:T(8,128)S(1)} fusion(f32[8,256,768]{1,2,0:T(8,128)S(1)} %bitcast_select_fusion, f32[5,96,768]{2,1,0:T(8,128)S(1)} %copy-done.7), kind=kOutput, calls=%fused_computation.27 | convolution fusion | flops 4529848320 | bytes 11698176 | tf_op jit(solution)/shard_map/btc,koc->kbto/dot_general | solution.py:68
  112.7 5.3 %collective-permute-start.18 = (f32[8,8,96]{1,2,0:T(8,128)S(1)}, f32[8,8,96]{1,2,0:T(8,128)S(1)}, u32[]{:S(2)}, u32[]{:S(2)}) collective-permute-start(f32[8,8,96]{1,2,0:T(8,128)S(1)} %get-tuple-element.32), channel_id=1, source_target_pairs={{0,8},{8,16},{16,24},{1,9},{9,17},{17,25},{2,10},{10,18},{18,26},{... | collective-permute-start | bytes 73736 | tf_op jit(solution)/shard_map/ppermute | solution.py:37
  118.0 7.1 %collective-permute-done.19 = f32[8,8,96]{1,2,0:T(8,128)S(1)} collective-permute-done((f32[8,8,96]{1,2,0:T(8,128)S(1)}, f32[8,8,96]{1,2,0:T(8,128)S(1)}, u32[]{:S(2)}, u32[]{:S(2)}) %collective-permute-start.19) | collective-permute-done | bytes 24608 | tf_op jit(solution)/shard_map/ppermute | solution.py:37
  127.4 11.7 %all_to_all.25 = f32[4,2,32,96]{3,2,1,0:T(8,128)S(1)} all-to-all(f32[4,2,32,96]{3,2,1,0:T(8,128)S(1)} %bitcast.160), channel_id=1, replica_groups=mesh['seq'=4,'crow'=4,'ccol'=2] {'seq'}, dimensions={0} | all-to-all | bytes 196608 | tf_op jit(solution)/shard_map/all_to_all | solution.py:151
  140.2 3.5 %all-to-all-start.1 = ((f32[8,2,128,96]{2,3,1,0:T(8,128)}), f32[8,2,128,96]{2,3,1,0:T(8,128)S(1)}, u32[]{:S(2)}, u32[]{:S(2)}) async-start(f32[8,2,128,96]{2,3,1,0:T(8,128)} %broadcast_in_dim.123), calls=%async_computation.1 | async-start | bytes 1572864 | tf_op jit(solution)/shard_map/all_to_all | solution.py:20
  145.2 11.1 %all-to-all-done.1 = f32[8,2,128,96]{2,3,1,0:T(8,128)S(1)} async-done(((f32[8,2,128,96]{2,3,1,0:T(8,128)}), f32[8,2,128,96]{2,3,1,0:T(8,128)S(1)}, u32[]{:S(2)}, u32[]{:S(2)}) %all-to-all-start.1) | async-done | bytes 786464 | tf_op jit(solution)/shard_map/all_to_all | solution.py:20
  158.8 3.6 %all-to-all-start.2 = ((f32[8,2,192,128]{3,2,1,0:T(8,128)}), f32[8,2,192,128]{3,2,1,0:T(8,128)S(1)}, u32[]{:S(2)}, u32[]{:S(2)}) async-start(f32[8,2,192,128]{3,2,1,0:T(8,128)} %broadcast_in_dim.125), calls=%async_computation.2 | async-start | bytes 3145728 | tf_op jit(solution)/shard_map/all_to_all | solution.py:20
  162.4 5.4 %copy.51 = f32[1536,576]{1,0:T(8,128)} copy(f32[1536,576]{0,1:T(8,128)} %param.26) | data formatting | bytes 7077888 | tf_op args[11]
  167.9 1.6 copy.75
  169.8 13.6 %all-to-all-done.2 = f32[8,2,192,128]{3,2,1,0:T(8,128)S(1)} async-done(((f32[8,2,192,128]{3,2,1,0:T(8,128)}), f32[8,2,192,128]{3,2,1,0:T(8,128)S(1)}, u32[]{:S(2)}, u32[]{:S(2)}) %all-to-all-start.2) | async-done | bytes 1572896 | tf_op jit(solution)/shard_map/all_to_all | solution.py:20
  183.7 1.8 reshape.140
  185.5 6.9 %fusion.18 = f32[2,128,576]{1,2,0:T(8,128)S(1)} fusion(f32[8,192,576,1]{2,1,3,0:T(8,128)} %bitcast.142, f32[8,2,128,192]{3,2,1,0:T(8,128)} %reshape.140, f32[8,192]{1,0:T(8,128)S(1)} %mul.194, f32[2,128]{1,0:T(2,128)S(1)} %add_sqrt_fusion), kind=kOutput, calls=%fused_computation.34 | convolution fusion | flops 1359495168 | bytes 5708800 | tf_op jit(solution)/shard_map/nbtj,njo->bto/dot_general | solution.py:134
  194.3 23.5 %all_to_all.26 = f32[8,2,128,192]{2,3,1,0:T(8,128)S(1)} all-to-all(f32[8,2,128,192]{2,3,1,0:T(8,128)S(1)} %copy.55), channel_id=1, replica_groups=mesh['seq'=4,'crow'=4,'ccol'=2] {'crow','ccol'}, dimensions={0} | all-to-all | bytes 3145728 | tf_op jit(solution)/shard_map/all_to_all | solution.py:172
  218.3 9.7 %all_to_all.27 = f32[4,2,48,128]{3,2,1,0:T(8,128)S(1)} all-to-all(f32[4,2,48,128]{3,2,1,0:T(8,128)S(1)} %copy.58), channel_id=1, replica_groups=mesh['seq'=4,'crow'=4,'ccol'=2] {'seq'}, dimensions={0} | all-to-all | bytes 393216 | tf_op jit(solution)/shard_map/all_to_all | solution.py:174
  (115 shorter events, 31.6 us)
Async XLA Ops:
  0.6 45.5 %copy-start = (f32[5,96,768]{2,1,0:T(8,128)S(1)}, f32[5,96,768]{2,1,0:T(8,128)}, u32[]{:S(2)}) copy-start(f32[5,96,768]{2,1,0:T(8,128)} %param.19) | copy-start | bytes 4423684
  0.6 40.1 %copy-start.2 = (f32[8,96,256]{2,1,0:T(8,128)S(1)}, f32[8,96,256]{2,1,0:T(8,128)}, u32[]{:S(2)}) copy-start(f32[8,96,256]{2,1,0:T(8,128)} %param.15) | copy-start | bytes 2359300
  0.7 40.1 %copy-start.10 = (f32[96]{0:T(128)S(1)}, f32[96]{0:T(128)}, u32[]{:S(2)}) copy-start(f32[96]{0:T(128)} %param.17) | copy-start | bytes 1156
  0.7 40.1 %copy-start.11 = (f32[96]{0:T(128)S(1)}, f32[96]{0:T(128)}, u32[]{:S(2)}) copy-start(f32[96]{0:T(128)} %param.16) | copy-start | bytes 1156
  4.6 20.7 %collective-permute-start = (f32[8,96,256]{2,1,0:T(8,128)}, f32[8,96,256]{2,1,0:T(8,128)S(1)}, u32[]{:S(2)}, u32[]{:S(2)}) collective-permute-start(f32[8,96,256]{2,1,0:T(8,128)} %fusion.36), channel_id=1, source_target_pairs={{0,2},{2,0},{4,6},{6,4},{1,3},{3,1},{5,7},{7,5},{8,10},{10,8},{12,... | collective-permute-start | bytes 2359304 | tf_op jit(solution)/shard_map/ppermute | solution.py:42
  7.6 20.3 %collective-permute-start.1 = (f32[8,96,256]{2,1,0:T(8,128)}, f32[8,96,256]{2,1,0:T(8,128)S(1)}, u32[]{:S(2)}, u32[]{:S(2)}) collective-permute-start(f32[8,96,256]{2,1,0:T(8,128)} %fusion.36), channel_id=1, source_target_pairs={{0,4},{2,6},{4,0},{6,2},{1,5},{3,7},{5,1},{7,3},{8,12},{10,14},{12... | collective-permute-start | bytes 2359304 | tf_op jit(solution)/shard_map/ppermute | solution.py:43
  26.1 10.5 %collective-permute-start.2 = (f32[4,96,256]{2,1,0:T(8,128)}, f32[4,96,256]{2,1,0:T(8,128)S(1)}, u32[]{:S(2)}, u32[]{:S(2)}) collective-permute-start(f32[4,96,256]{2,1,0:T(8,128)} %slice.117), channel_id=1, source_target_pairs={{0,4},{2,6},{4,0},{6,2},{1,5},{3,7},{5,1},{7,3},{8,12},{10,14},{12... | collective-permute-start | bytes 1179656 | tf_op jit(solution)/shard_map/ppermute | solution.py:45
  29.6 10.0 %collective-permute-start.3 = (f32[4,96,256]{2,1,0:T(8,128)}, f32[4,96,256]{2,1,0:T(8,128)}, u32[]{:S(2)}, u32[]{:S(2)}) collective-permute-start(f32[4,96,256]{2,1,0:T(8,128)} %slice.118), channel_id=1, source_target_pairs={{0,2},{2,0},{4,6},{6,4},{1,3},{3,1},{5,7},{7,5},{8,10},{10,8},{12,... | collective-permute-start | bytes 1179656 | tf_op jit(solution)/shard_map/ppermute | solution.py:46
  31.1 12.1 %collective-permute-start.4 = (f32[8,96,256]{2,1,0:T(8,128)}, f32[8,96,256]{2,1,0:T(8,128)}, u32[]{:S(2)}, u32[]{:S(2)}) collective-permute-start(f32[8,96,256]{2,1,0:T(8,128)} %fusion.36), channel_id=1, source_target_pairs={{0,1},{1,0},{2,3},{3,2},{4,5},{5,4},{6,7},{7,6},{8,9},{9,8},{10,11... | collective-permute-start | bytes 2359304 | tf_op jit(solution)/shard_map/ppermute | solution.py:28
  31.2 11.9 %collective-permute-start.6 = (f32[8,96,256]{2,1,0:T(8,128)}, f32[8,96,256]{2,1,0:T(8,128)S(1)}, u32[]{:S(2)}, u32[]{:S(2)}) collective-permute-start(f32[8,96,256]{2,1,0:T(8,128)} %copy-done.5), channel_id=1, source_target_pairs={{0,1},{1,0},{2,3},{3,2},{4,5},{5,4},{6,7},{7,6},{8,9},{9,8},{10,11... | collective-permute-start | bytes 2359304 | tf_op jit(solution)/shard_map/ppermute | solution.py:28
  31.8 11.4 %collective-permute-start.5 = (f32[8,96,256]{2,1,0:T(8,128)S(1)}, f32[8,96,256]{2,1,0:T(8,128)S(1)}, u32[]{:S(2)}, u32[]{:S(2)}) collective-permute-start(f32[8,96,256]{2,1,0:T(8,128)S(1)} %collective-permute-done), channel_id=1, source_target_pairs={{0,1},{1,0},{2,3},{3,2},{4,5},{5,4},{6,7},{7,6},{8,9},{9,8},{10,11... | collective-permute-start | bytes 2359304 | tf_op jit(solution)/shard_map/ppermute | solution.py:28
  40.6 2.5 %collective-permute-start.7 = (f32[8,96,256]{2,1,0:T(8,128)S(1)}, f32[8,96,256]{2,1,0:T(8,128)S(1)}, u32[]{:S(2)}, u32[]{:S(2)}) collective-permute-start(f32[8,96,256]{2,1,0:T(8,128)S(1)} %constant_dynamic-update-slice_fusion), channel_id=1, source_target_pairs={{0,1},{1,0},{2,3},{3,2},{4,5},{5,4},{6,7},{7,6},{8,9},{9,8},{10,11... | collective-permute-start | bytes 2359304 | tf_op jit(solution)/shard_map/ppermute | solution.py:28
  51.6 16.2 %copy-start.13 = (f32[96]{0:T(128)S(1)}, f32[96]{0:T(128)}, u32[]{:S(2)}) copy-start(f32[96]{0:T(128)} %param.21) | copy-start | bytes 1156
  51.7 16.2 %copy-start.14 = (f32[96]{0:T(128)S(1)}, f32[96]{0:T(128)}, u32[]{:S(2)}) copy-start(f32[96]{0:T(128)} %param.20) | copy-start | bytes 1156
  51.7 16.2 %copy-start.15 = (f32[96]{0:T(128)S(1)}, f32[96]{0:T(128)}, u32[]{:S(2)}) copy-start(f32[96]{0:T(128)} %param.18) | copy-start | bytes 1156
  53.3 13.4 %collective-permute-start.9 = (f32[8,4,96]{1,2,0:T(8,128)S(1)}, f32[8,4,96]{1,2,0:T(8,128)S(1)}, u32[]{:S(2)}, u32[]{:S(2)}) collective-permute-start(f32[8,4,96]{1,2,0:T(8,128)S(1)} %get-tuple-element.35), channel_id=1, source_target_pairs={{8,0},{16,8},{24,16},{9,1},{17,9},{25,17},{10,2},{18,10},{26,18},{... | collective-permute-start | bytes 36872 | tf_op jit(solution)/shard_map/ppermute | solution.py:37
  54.6 13.3 %collective-permute-start.8 = (f32[8,4,96]{1,2,0:T(8,128)S(1)}, f32[8,4,96]{1,2,0:T(8,128)S(1)}, u32[]{:S(2)}, u32[]{:S(2)}) collective-permute-start(f32[8,4,96]{1,2,0:T(8,128)S(1)} %get-tuple-element.34), channel_id=1, source_target_pairs={{0,8},{8,16},{16,24},{1,9},{9,17},{17,25},{2,10},{10,18},{18,26},{... | collective-permute-start | bytes 36872 | tf_op jit(solution)/shard_map/ppermute | solution.py:37
  69.9 18.9 %collective-permute-start.10 = (f32[8,96,256]{2,1,0:T(8,128)S(1)}, f32[8,96,256]{2,1,0:T(8,128)S(1)}, u32[]{:S(2)}, u32[]{:S(2)}) collective-permute-start(f32[8,96,256]{2,1,0:T(8,128)S(1)} %get-tuple-element.14), channel_id=1, source_target_pairs={{0,2},{2,0},{4,6},{6,4},{1,3},{3,1},{5,7},{7,5},{8,10},{10,8},{12,... | collective-permute-start | bytes 2359304 | tf_op jit(solution)/shard_map/ppermute | solution.py:42
  71.4 18.6 %collective-permute-start.11 = (f32[8,96,256]{2,1,0:T(8,128)S(1)}, f32[8,96,256]{2,1,0:T(8,128)S(1)}, u32[]{:S(2)}, u32[]{:S(2)}) collective-permute-start(f32[8,96,256]{2,1,0:T(8,128)S(1)} %get-tuple-element.14), channel_id=1, source_target_pairs={{0,4},{2,6},{4,0},{6,2},{1,5},{3,7},{5,1},{7,3},{8,12},{10,14},{12... | collective-permute-start | bytes 2359304 | tf_op jit(solution)/shard_map/ppermute | solution.py:43
  88.8 9.6 %collective-permute-start.12 = (f32[4,96,256]{2,1,0:T(8,128)S(1)}, f32[4,96,256]{2,1,0:T(8,128)S(1)}, u32[]{:S(2)}, u32[]{:S(2)}) collective-permute-start(f32[4,96,256]{2,1,0:T(8,128)S(1)} %slice.122), channel_id=1, source_target_pairs={{0,4},{2,6},{4,0},{6,2},{1,5},{3,7},{5,1},{7,3},{8,12},{10,14},{12... | collective-permute-start | bytes 1179656 | tf_op jit(solution)/shard_map/ppermute | solution.py:45
  90.0 9.2 %collective-permute-start.13 = (f32[4,96,256]{2,1,0:T(8,128)S(1)}, f32[4,96,256]{2,1,0:T(8,128)S(1)}, u32[]{:S(2)}, u32[]{:S(2)}) collective-permute-start(f32[4,96,256]{2,1,0:T(8,128)S(1)} %slice.123), channel_id=1, source_target_pairs={{0,2},{2,0},{4,6},{6,4},{1,3},{3,1},{5,7},{7,5},{8,10},{10,8},{12,... | collective-permute-start | bytes 1179656 | tf_op jit(solution)/shard_map/ppermute | solution.py:46
  90.9 8.7 %collective-permute-start.14 = (f32[8,96,256]{2,1,0:T(8,128)S(1)}, f32[8,96,256]{2,1,0:T(8,128)S(1)}, u32[]{:S(2)}, u32[]{:S(2)}) collective-permute-start(f32[8,96,256]{2,1,0:T(8,128)S(1)} %get-tuple-element.14), channel_id=1, source_target_pairs={{0,1},{1,0},{2,3},{3,2},{4,5},{5,4},{6,7},{7,6},{8,9},{9,8},{10,11... | collective-permute-start | bytes 2359304 | tf_op jit(solution)/shard_map/ppermute | solution.py:28
  90.9 8.7 %collective-permute-start.16 = (f32[8,96,256]{2,1,0:T(8,128)S(1)}, f32[8,96,256]{2,1,0:T(8,128)S(1)}, u32[]{:S(2)}, u32[]{:S(2)}) collective-permute-start(f32[8,96,256]{2,1,0:T(8,128)S(1)} %collective-permute-done.11), channel_id=1, source_target_pairs={{0,1},{1,0},{2,3},{3,2},{4,5},{5,4},{6,7},{7,6},{8,9},{9,8},{10,11... | collective-permute-start | bytes 2359304 | tf_op jit(solution)/shard_map/ppermute | solution.py:28
  91.4 8.2 %collective-permute-start.15 = (f32[8,96,256]{2,1,0:T(8,128)S(1)}, f32[8,96,256]{2,1,0:T(8,128)S(1)}, u32[]{:S(2)}, u32[]{:S(2)}) collective-permute-start(f32[8,96,256]{2,1,0:T(8,128)S(1)} %collective-permute-done.10), channel_id=1, source_target_pairs={{0,1},{1,0},{2,3},{3,2},{4,5},{5,4},{6,7},{7,6},{8,9},{9,8},{10,11... | collective-permute-start | bytes 2359304 | tf_op jit(solution)/shard_map/ppermute | solution.py:28
  99.3 2.4 %collective-permute-start.17 = (f32[8,96,256]{2,1,0:T(8,128)S(1)}, f32[8,96,256]{2,1,0:T(8,128)S(1)}, u32[]{:S(2)}, u32[]{:S(2)}) collective-permute-start(f32[8,96,256]{2,1,0:T(8,128)S(1)} %constant_dynamic-update-slice_fusion.2), channel_id=1, source_target_pairs={{0,1},{1,0},{2,3},{3,2},{4,5},{5,4},{6,7},{7,6},{8,9},{9,8},{10,11... | collective-permute-start | bytes 2359304 | tf_op jit(solution)/shard_map/ppermute | solution.py:28
  109.9 16.4 %copy-start.12 = (f32[96]{0:T(128)S(1)}, f32[96]{0:T(128)}, u32[]{:S(2)}) copy-start(f32[96]{0:T(128)} %param.22) | copy-start | bytes 1156
  111.4 13.8 %collective-permute-start.19 = (f32[8,8,96]{1,2,0:T(8,128)S(1)}, f32[8,8,96]{1,2,0:T(8,128)S(1)}, u32[]{:S(2)}, u32[]{:S(2)}) collective-permute-start(f32[8,8,96]{1,2,0:T(8,128)S(1)} %get-tuple-element.33), channel_id=1, source_target_pairs={{8,0},{16,8},{24,16},{9,1},{17,9},{25,17},{10,2},{18,10},{26,18},{... | collective-permute-start | bytes 73736 | tf_op jit(solution)/shard_map/ppermute | solution.py:37
  112.7 13.7 %collective-permute-start.18 = (f32[8,8,96]{1,2,0:T(8,128)S(1)}, f32[8,8,96]{1,2,0:T(8,128)S(1)}, u32[]{:S(2)}, u32[]{:S(2)}) collective-permute-start(f32[8,8,96]{1,2,0:T(8,128)S(1)} %get-tuple-element.32), channel_id=1, source_target_pairs={{0,8},{8,16},{16,24},{1,9},{9,17},{17,25},{2,10},{10,18},{18,26},{... | collective-permute-start | bytes 73736 | tf_op jit(solution)/shard_map/ppermute | solution.py:37
  126.8 18.4 %copy-start.4 = (f32[8,96,256]{2,1,0:T(8,128)}, f32[8,96,256]{2,1,0:T(8,128)S(1)}, u32[]{:S(2)}) copy-start(f32[8,96,256]{2,1,0:T(8,128)S(1)} %fusion.40) | copy-start | bytes 2359300
  140.2 16.1 %all-to-all-start.1 = ((f32[8,2,128,96]{2,3,1,0:T(8,128)}), f32[8,2,128,96]{2,3,1,0:T(8,128)S(1)}, u32[]{:S(2)}, u32[]{:S(2)}) async-start(f32[8,2,128,96]{2,3,1,0:T(8,128)} %broadcast_in_dim.123), calls=%async_computation.1 | async-start | bytes 1572864 | tf_op jit(solution)/shard_map/all_to_all | solution.py:20
  158.8 24.5 %all-to-all-start.2 = ((f32[8,2,192,128]{3,2,1,0:T(8,128)}), f32[8,2,192,128]{3,2,1,0:T(8,128)S(1)}, u32[]{:S(2)}, u32[]{:S(2)}) async-start(f32[8,2,192,128]{3,2,1,0:T(8,128)} %broadcast_in_dim.125), calls=%async_computation.2 | async-start | bytes 3145728 | tf_op jit(solution)/shard_map/all_to_all | solution.py:20
  194.2 34.6 %copy-start.1 = (f32[5,96,768]{2,1,0:T(8,128)S(1)}, f32[5,96,768]{2,1,0:T(8,128)}, u32[]{:S(2)}) copy-start(f32[5,96,768]{2,1,0:T(8,128)} %param.19) | copy-start | bytes 4423684
  (6 other events, 32.3 us)
